TPU v7x, 512 devices: a whole 4x4x16 slice. The times are simulated.
512 devices in a mesh: seq: 128 (over y, x, z_hi, core), ch: 4 (over z_lo).
Axes of the slice: x: 4, y: 4, z: 16 (z_hi: 4, z_lo: 4; z = z_hi * 4 + z_lo), core: 2. Of those that a mesh axis runs over, the one named last changes fastest.
Arguments:
- signal: bfloat16 [256, 32768], P('ch', 'seq'), may hold values from -400 to 400
- long_filter: float32 [256, 32768], P('ch', 'seq'), may hold values from -1.8 to 1.8
- skip_weight: float32 [256], P('ch'), may hold values from 0.5 to 1.5
- short_taps: float32 [7, 256], P(None, 'ch'), may hold values from -2 to 2
- norm_gain: float32 [256], P('ch'), may hold values from 0.5 to 1.5
Outputs:
- normed: float32 [256, 32768], P('ch', 'seq')
All inputs are finite; a program needn't handle non-finite values.
Results may differ from a plain program's by a relative error of at most 0.0003.
Values sent between devices are 32-bit elements; how exact they have to be, the bound alone decides.
No kernel may reach another device: no remote copies, remote signals or barrier semaphores. Data moves between devices by JAX's collectives and lax.ppermute only.
A program may use at most 64 MiB of HBM per device.

v0:
```python
import math

import jax
import jax.numpy as jnp
from jax import lax
from jax.sharding import PartitionSpec as P

highest = lax.Precision.HIGH


def phases(left_ids, right_ids, modulus, direction):
    product = left_ids[:, None] * right_ids[None, :] % modulus
    angles = product.astype(jnp.float32) * (2.0 * math.pi / modulus)
    return (jnp.cos(angles), direction * jnp.sin(angles))


def mat(a, b):
    return jnp.dot(a, b, precision=highest, preferred_element_type=jnp.float32)


def cmat(ar, ai, br, bi):
    if ai is None:
        return (mat(ar, br), mat(ar, bi))
    if bi is None:
        return (mat(ar, br), mat(ai, br))
    return (mat(ar, br) - mat(ai, bi), mat(ar, bi) + mat(ai, br))


def cmul(ar, ai, br, bi):
    return (ar * br - ai * bi, ar * bi + ai * br)


def local(signal, long_filter, skip_weight, short_taps, norm_gain):
    seq_parts = lax.axis_size("seq")
    width, length = signal.shape
    dup = seq_parts // width
    piece = length // dup
    own = lax.axis_index("seq")
    chan = own // dup
    half = own % dup
    signal_f = signal.astype(jnp.float32)

    both = jnp.stack([signal_f, long_filter], 1)
    send = jnp.repeat(both, dup, axis=0)
    recv = lax.all_to_all(send, "seq", 0, 0, tiled=True)
    x_rows = recv[:, 0, :]
    h_rows = recv[:, 1, :]

    rows = 2 * seq_parts
    cols = length
    modulus = rows * cols
    row_ids = jnp.arange(rows, dtype=jnp.int32)
    col_ids = jnp.arange(cols, dtype=jnp.int32)
    square = phases(col_ids, col_ids, cols, 1.0)
    turn = phases(row_ids, col_ids, modulus, 1.0)
    square, turn = lax.optimization_barrier((square, turn))
    rows_fwd = (square[0][:, :seq_parts], -square[1][:, :seq_parts])
    turn_fwd = (turn[0], -turn[1])
    cols_fwd = (square[0], -square[1])
    cols_inv = square
    rows_inv = (square[0][:seq_parts], square[1][:seq_parts])

    def forward(x):
        yr, yi = cmat(rows_fwd[0], rows_fwd[1], x, None)
        yr, yi = cmul(yr, yi, turn_fwd[0], turn_fwd[1])
        return cmat(yr, yi, cols_fwd[0], cols_fwd[1])

    xr, xi = forward(x_rows)
    hr, hi = forward(h_rows)
    pr, pi = cmul(xr, xi, hr, hi)
    qr, qi = cmat(pr, pi, cols_inv[0], cols_inv[1])
    qr, qi = cmul(qr, qi, turn_fwd[0], -turn_fwd[1])
    conv = (mat(rows_inv[0], qr) - mat(rows_inv[1], qi)) * (1.0 / modulus)

    skip = lax.dynamic_index_in_dim(skip_weight, chan, keepdims=False)
    mixed = (conv + skip * x_rows).reshape(seq_parts * length)
    tap_count = short_taps.shape[0]
    taps = lax.dynamic_index_in_dim(short_taps, chan, axis=1, keepdims=False)
    padded = jnp.concatenate([jnp.zeros((tap_count - 1,), mixed.dtype), mixed])
    total = seq_parts * length
    short = jnp.zeros_like(mixed)
    for offset in range(tap_count):
        start = tap_count - 1 - offset
        short = short + taps[offset] * padded[start : start + total]
    short_rows = short.reshape(seq_parts, length)
    back = lax.dynamic_slice_in_dim(short_rows, half * piece, piece, axis=1)
    got = lax.all_to_all(back, "seq", 0, 0, tiled=True)
    short_local = got.reshape(width, length)

    energy = lax.psum(jnp.sum(short_local * short_local, 0), "ch")
    all_channels = width * lax.axis_size("ch")
    return short_local * norm_gain[:, None] * lax.rsqrt(energy / all_channels + 1e-06)[None, :]


def solution(mesh):
    return jax.shard_map(
        local,
        mesh=mesh,
        in_specs=(P("ch", "seq"), P("ch", "seq"), P("ch"), P(None, "ch"), P("ch")),
        out_specs=P("ch", "seq"),
        check_vma=False,
    )
```

profile of v0, /device:TPU:1, one launch (start us, length us, event | category | flops | bytes accessed | tf_op | source)
XLA Modules:
  0.0 95.3 jit_solution(8321526033220471262)
XLA Ops:
  0.0 0.8 bitcast_convert_fusion
  1.0 0.8 broadcast_in_dim.2
  1.8 23.0 %all-to-all-start = ((f32[128,2,256]{2,1,0:T(2,128)}), f32[128,2,256]{2,1,0:T(2,128)S(1)}, u32[]{:S(2)}, u32[]{:S(2)}) async-start(f32[128,2,256]{2,1,0:T(2,128)} %bitcast.3), calls=%async_computation | async-start | bytes 524288 | tf_op jit(solution)/shard_map/all_to_all | solution.py:45
  24.8 1.0 %fusion.34 = (f32[256,256]{1,0:T(8,128)S(1)}, f32[256,256]{1,0:T(8,128)S(1)}) fusion(), kind=kLoop, calls=%fused_computation.62 | loop fusion | flops 917504 | bytes 524288 | tf_op jit(solution)/shard_map/sin | solution.py:14
  25.9 1.0 %fusion.32 = (f32[256,256]{1,0:T(8,128)S(1)}, f32[256,256]{1,0:T(8,128)S(1)}) fusion(), kind=kLoop, calls=%fused_computation.60 | loop fusion | flops 917504 | bytes 524288 | tf_op jit(solution)/shard_map/sin | solution.py:14
  26.9 0.6 copy-done.3
  27.6 0.6 dynamic_slice.12
  28.3 0.6 fusion.43
  28.9 18.0 %all-to-all-done = f32[128,2,256]{2,1,0:T(2,128)S(1)} async-done(((f32[128,2,256]{2,1,0:T(2,128)}), f32[128,2,256]{2,1,0:T(2,128)S(1)}, u32[]{:S(2)}, u32[]{:S(2)}) %all-to-all-start) | async-done | bytes 262176 | tf_op jit(solution)/shard_map/all_to_all | solution.py:45
  47.1 0.3 fusion.28
  47.9 0.3 multiply_add_fusion.1
  48.2 0.3 fusion.20
  48.5 0.3 fusion.45
  48.7 0.3 fusion.22
  49.0 0.3 fusion.44
  49.3 0.3 convolution_subtract_fusion.1
  49.6 0.3 convolution_add_fusion.1
  49.9 0.3 convolution_subtract_fusion.2
  50.2 0.3 multiply_add_fusion
  50.5 0.3 fusion.47
  50.8 0.3 fusion.46
  51.1 0.3 convolution_add_fusion
  51.3 0.3 convolution_subtract_fusion
  51.6 0.3 fusion.9
  51.9 1.6 %broadcast_multiply_fusion = (f32[128,256]{1,0:T(8,128)S(1)}, f32[128,256]{1,0:T(8,128)S(1)}) fusion(f32[]{:T(128)} %bitcast, f32[128,1,256]{2,1,0:T(1,128)S(1)} %get-tuple-element.22, f32[]{:T(128)} %bitcast.5, f32[128,256]{1,0:T(8,128)S(1)} %fusion.9, f32[256,256]{1,0:T(8,128)S(1)} %convolution_add_fusion, f32[256,256]{1,0:T(8,128)S(1)} %get-tuple-element.10, ...), kind=kOutput, calls=%fused_computation.78 | convolution fusion | flops 50692096 | bytes 1703944 | tf_op jit(solution)/shard_map/dot_general | solution.py:18
  53.5 4.0 %slice_multiply_fusion.5 = (f32[32768]{0:T(1024)S(1)}, f32[32768]{0:T(1024)S(1)}, f32[32768]{0:T(1024)S(1)}, f32[32768]{0:T(1024)S(1)}, f32[32768]{0:T(1024)S(1)}, /*index=5*/f32[32768]{0:T(1024)S(1)}) fusion(f32[32768]{0:T(1024)S(1)} %bitcast.50, f32[]{:T(128)} %bitcast.6, f32[]{:T(128)} %bitcast.7, f32[]{:T(128)} %bitcast.8, f32[]{:T(128)} %bitcast.9, ...), kind=kLoop, calls=%fused_computation.56 | loop fusion | flops 196608 | bytes 917528 | tf_op jit(solution)/shard_map/mul | solution.py:84
  57.9 26.3 %all_to_all.14 = f32[128,1,128]{2,1,0:T(1,128)S(1)} all-to-all(f32[128,1,128]{2,1,0:T(1,128)S(1)} %bitcast.51), channel_id=1, replica_groups=mesh['seq'=128,'ch'=4] {'seq'}, dimensions={0} | all-to-all | bytes 131072 | tf_op jit(solution)/shard_map/all_to_all | solution.py:87
  84.2 0.5 broadcast.50
  84.7 0.8 reduce.3
  85.5 8.4 %psum.7 = f32[256]{0:T(256)S(1)} all-reduce(f32[256]{0:T(256)S(1)} %multiply_reduce_fusion), channel_id=1, replica_groups=mesh['seq'=128,'ch'=4] {'ch'}, use_global_device_ids=true, to_apply=%region_1.2 | all-reduce | flops 256 | bytes 2048 | tf_op jit(solution)/shard_map/psum | solution.py:90
  94.0 0.6 copy-done.2
  94.6 0.7 multiply_multiply_fusion
  (23 shorter events, 1.4 us)
Async XLA Ops:
  0.0 28.2 %copy-start = (f32[7,64]{1,0:T(8,128)S(1)}, f32[7,64]{1,0:T(8,128)}, u32[]{:S(2)}) copy-start(f32[7,64]{1,0:T(8,128)} %param.8) | copy-start | bytes 5380
  0.0 0.9 copy-start.1
  1.8 45.1 %all-to-all-start = ((f32[128,2,256]{2,1,0:T(2,128)}), f32[128,2,256]{2,1,0:T(2,128)S(1)}, u32[]{:S(2)}, u32[]{:S(2)}) async-start(f32[128,2,256]{2,1,0:T(2,128)} %bitcast.3), calls=%async_computation | async-start | bytes 524288 | tf_op jit(solution)/shard_map/all_to_all | solution.py:45
  26.9 0.7 copy-start.3
  94.0 0.7 copy-start.2
where the time goes:
time: 96 us; the launch traced here: 95.3 us
  blocking collectives  34.7 us (36%)
  starting transfers between devices  23 us (24%)
  waiting for transfers between devices  18 us (19%)
  other arithmetic  8.48 us (9%)
  matrix products  6.24 us (6%)
  local copies, waits for them, and re-layouts  4.6 us (5%)
    all_to_all x1, blocking collectives, local(): got = lax.all_to_all(back, 'seq', 0, 0, tiled=True)  26.3 us
    all_to_all x1, starting transfers between devices, local(): recv = lax.all_to_all(send, 'seq', 0, 0, tiled=True)  23 us
    all_to_all x1, waiting for transfers between devices, local(): recv = lax.all_to_all(send, 'seq', 0, 0, tiled=True)  18 us
    psum x1, blocking collectives, local(): energy = lax.psum(jnp.sum(short_local * short_local, 0), 'ch')  8.44 us
    dot_general x18, matrix products, mat(): return jnp.dot(a, b, precision=highest, preferred_element_type=jnp.float32)  6.24 us
    mul x1, other arithmetic, local(): short = short + taps[offset] * padded[start:start + total]  4.02 us
    sin x2, other arithmetic, phases(): return (jnp.cos(angles), direction * jnp.sin(angles))  2.07 us
  transfers between devices with their start and end apart: 1, of which 1 were waited for; matrix products, arithmetic and copies ran while one was open for 4% of the time, Pallas kernels for 0%

commit v1 on v0

--- a/solution.py
+++ b/solution.py
@@ -84,11 +84,13 @@
         short = short + taps[offset] * padded[start : start + total]
     short_rows = short.reshape(seq_parts, length)
     back = lax.dynamic_slice_in_dim(short_rows, half * piece, piece, axis=1)
-    got = lax.all_to_all(back, "seq", 0, 0, tiled=True)
-    short_local = got.reshape(width, length)
-
-    energy = lax.psum(jnp.sum(short_local * short_local, 0), "ch")
-    all_channels = width * lax.axis_size("ch")
+    groups = lax.axis_size("ch")
+    spread = jnp.tile(back, (groups, 1))
+    got = lax.all_to_all(spread, ("ch", "seq"), 0, 0, tiled=True)
+    every = got.reshape(groups, width, length)
+    energy = jnp.sum(every * every, (0, 1))
+    short_local = lax.dynamic_index_in_dim(every, lax.axis_index("ch"), keepdims=False)
+    all_channels = width * groups
     return short_local * norm_gain[:, None] * lax.rsqrt(energy / all_channels + 1e-06)[None, :]
 
 

time: 96 us -> 96.7 us (level)
  blocking collectives: 34.7 us -> 0 us
  waiting for transfers between devices: 18 us -> 41.4 us
  starting transfers between devices: 23 us -> 34.1 us
    all_to_all x1 -> x0, blocking collectives: 26.3 us -> none  [local(): got = lax.all_to_all(back, 'seq', 0, 0, tiled=True)]
    all_to_all x0 -> x1, waiting for transfers between devices: none -> 23.3 us  [local(): got = lax.all_to_all(spread, ('ch', 'seq'), 0, 0, tiled=True)]
    all_to_all x0 -> x1, starting transfers between devices: none -> 11.1 us  [local(): got = lax.all_to_all(spread, ('ch', 'seq'), 0, 0, tiled=True)]
    psum x1 -> x0, blocking collectives: 8.44 us -> none  [local(): energy = lax.psum(jnp.sum(short_local * short_local, 0), 'ch')]
  transfers between devices with their start and end apart: 1 -> 2, of which waited for: 1 -> 2; matrix products, arithmetic and copies ran while one was open for 4% -> 3% of each run, Pallas kernels for 0% -> 0%
where the time goes in v1:
time: 96.7 us; the launch traced here: 96.3 us
  waiting for transfers between devices  41.4 us (43%)
  starting transfers between devices  34.1 us (35%)
  other arithmetic  9.06 us (9%)
  matrix products  6.13 us (6%)
  local copies, waits for them, and re-layouts  5.33 us (6%)
    all_to_all x1, waiting for transfers between devices, local(): got = lax.all_to_all(spread, ('ch', 'seq'), 0, 0, tiled=True)  23.3 us
    all_to_all x1, starting transfers between devices, local(): recv = lax.all_to_all(send, 'seq', 0, 0, tiled=True)  23 us
    all_to_all x1, waiting for transfers between devices, local(): recv = lax.all_to_all(send, 'seq', 0, 0, tiled=True)  18 us
    all_to_all x1, starting transfers between devices, local(): got = lax.all_to_all(spread, ('ch', 'seq'), 0, 0, tiled=True)  11.1 us
    dot_general x18, matrix products, mat(): return jnp.dot(a, b, precision=highest, preferred_element_type=jnp.float32)  6.13 us
    mul x1, other arithmetic, local(): short = short + taps[offset] * padded[start:start + total]  4.12 us
    sin x2, other arithmetic, phases(): return (jnp.cos(angles), direction * jnp.sin(angles))  2.07 us
  transfers between devices with their start and end apart: 2, of which 2 were waited for; matrix products, arithmetic and copies ran while one was open for 3% of the time, Pallas kernels for 0%

profile of v1, /device:TPU:1, one launch (start us, length us, event | category | flops | bytes accessed | tf_op | source)
XLA Modules:
  0.0 96.3 jit_solution(9704100836913526890)
XLA Ops:
  0.0 0.8 bitcast_convert_fusion
  1.0 0.8 broadcast_in_dim.2
  1.8 23.0 %all-to-all-start = ((f32[128,2,256]{2,1,0:T(2,128)}), f32[128,2,256]{2,1,0:T(2,128)S(1)}, u32[]{:S(2)}, u32[]{:S(2)}) async-start(f32[128,2,256]{2,1,0:T(2,128)} %bitcast.3), calls=%async_computation | async-start | bytes 524288 | tf_op jit(solution)/shard_map/all_to_all | solution.py:45
  24.8 1.0 %fusion.34 = (f32[256,256]{1,0:T(8,128)S(1)}, f32[256,256]{1,0:T(8,128)S(1)}) fusion(), kind=kLoop, calls=%fused_computation.63 | loop fusion | flops 917504 | bytes 524288 | tf_op jit(solution)/shard_map/sin | solution.py:14
  25.9 1.0 %fusion.32 = (f32[256,256]{1,0:T(8,128)S(1)}, f32[256,256]{1,0:T(8,128)S(1)}) fusion(), kind=kLoop, calls=%fused_computation.61 | loop fusion | flops 917504 | bytes 524288 | tf_op jit(solution)/shard_map/sin | solution.py:14
  26.9 0.6 copy-done.3
  27.6 0.6 dynamic_slice.16
  28.2 0.6 fusion.44
  28.9 18.0 %all-to-all-done = f32[128,2,256]{2,1,0:T(2,128)S(1)} async-done(((f32[128,2,256]{2,1,0:T(2,128)}), f32[128,2,256]{2,1,0:T(2,128)S(1)}, u32[]{:S(2)}, u32[]{:S(2)}) %all-to-all-start) | async-done | bytes 262176 | tf_op jit(solution)/shard_map/all_to_all | solution.py:45
  47.9 0.3 multiply_add_fusion.1
  48.2 0.3 fusion.20
  48.5 0.3 fusion.46
  48.8 0.3 fusion.22
  49.1 0.3 fusion.45
  49.3 0.3 convolution_subtract_fusion.1
  49.6 0.3 convolution_add_fusion.1
  49.9 0.3 convolution_subtract_fusion.2
  50.2 0.3 multiply_add_fusion
  50.5 0.3 fusion.48
  50.8 0.3 fusion.47
  51.1 0.3 convolution_add_fusion
  51.4 0.3 convolution_subtract_fusion
  51.6 0.3 fusion.9
  51.9 1.5 %broadcast_multiply_fusion = (f32[128,256]{1,0:T(8,128)S(1)}, f32[128,256]{1,0:T(8,128)S(1)}) fusion(f32[]{:T(128)} %bitcast, f32[128,1,256]{2,1,0:T(1,128)S(1)} %get-tuple-element.22, f32[]{:T(128)} %bitcast.5, f32[128,256]{1,0:T(8,128)S(1)} %fusion.9, f32[256,256]{1,0:T(8,128)S(1)} %convolution_add_fusion, f32[256,256]{1,0:T(8,128)S(1)} %get-tuple-element.10, ...), kind=kOutput, calls=%fused_computation.79 | convolution fusion | flops 50692096 | bytes 1703944 | tf_op jit(solution)/shard_map/dot_general | solution.py:18
  53.5 4.1 %slice_multiply_fusion.5 = (f32[32768]{0:T(1024)S(1)}, f32[32768]{0:T(1024)S(1)}, f32[32768]{0:T(1024)S(1)}, f32[32768]{0:T(1024)S(1)}, f32[32768]{0:T(1024)S(1)}, /*index=5*/f32[32768]{0:T(1024)S(1)}) fusion(f32[32768]{0:T(1024)S(1)} %bitcast.54, f32[]{:T(128)} %bitcast.6, f32[]{:T(128)} %bitcast.7, f32[]{:T(128)} %bitcast.8, f32[]{:T(128)} %bitcast.9, ...), kind=kLoop, calls=%fused_computation.57 | loop fusion | flops 196608 | bytes 917528 | tf_op jit(solution)/shard_map/mul | solution.py:84
  57.9 0.7 tile.2
  58.6 11.1 %all-to-all-start.1 = ((f32[512,1,128]{2,1,0:T(1,128)}), f32[512,1,128]{2,1,0:T(1,128)S(1)}, u32[]{:S(2)}, u32[]{:S(2)}) async-start(f32[512,1,128]{2,1,0:T(1,128)} %bitcast.12), calls=%async_computation.1 | async-start | bytes 524288 | tf_op jit(solution)/shard_map/all_to_all | solution.py:89
  69.7 23.3 %all-to-all-done.1 = f32[512,1,128]{2,1,0:T(1,128)S(1)} async-done(((f32[512,1,128]{2,1,0:T(1,128)}), f32[512,1,128]{2,1,0:T(1,128)S(1)}, u32[]{:S(2)}, u32[]{:S(2)}) %all-to-all-start.1) | async-done | bytes 262176 | tf_op jit(solution)/shard_map/all_to_all | solution.py:89
  93.0 0.5 broadcast.60
  93.6 1.3 %reduce.3 = f32[512,128]{1,0:T(8,128)S(1)} reduce(f32[512,1,128]{2,1,0:T(1,128)S(1)} %all-to-all-done.1, f32[]{:T(128)} %broadcast.60), dimensions={1}, to_apply=%all_to_all.11.reduce_sub_computation.3 | reduce | bytes 524292 | tf_op jit(solution)/shard_map/all_to_all | solution.py:89
  95.0 0.6 copy-done.2
  95.6 0.7 fusion.42
  (24 shorter events, 1.7 us)
Async XLA Ops:
  0.0 28.2 %copy-start = (f32[7,64]{1,0:T(8,128)S(1)}, f32[7,64]{1,0:T(8,128)}, u32[]{:S(2)}) copy-start(f32[7,64]{1,0:T(8,128)} %param.8) | copy-start | bytes 5380
  0.0 0.9 copy-start.1
  1.8 45.1 %all-to-all-start = ((f32[128,2,256]{2,1,0:T(2,128)}), f32[128,2,256]{2,1,0:T(2,128)S(1)}, u32[]{:S(2)}, u32[]{:S(2)}) async-start(f32[128,2,256]{2,1,0:T(2,128)} %bitcast.3), calls=%async_computation | async-start | bytes 524288 | tf_op jit(solution)/shard_map/all_to_all | solution.py:45
  26.9 0.7 copy-start.3
  58.6 34.4 %all-to-all-start.1 = ((f32[512,1,128]{2,1,0:T(1,128)}), f32[512,1,128]{2,1,0:T(1,128)S(1)}, u32[]{:S(2)}, u32[]{:S(2)}) async-start(f32[512,1,128]{2,1,0:T(1,128)} %bitcast.12), calls=%async_computation.1 | async-start | bytes 524288 | tf_op jit(solution)/shard_map/all_to_all | solution.py:89
  95.0 0.7 copy-start.2

commit v2 on v0

--- a/solution.py
+++ b/solution.py
@@ -73,17 +73,17 @@
     conv = (mat(rows_inv[0], qr) - mat(rows_inv[1], qi)) * (1.0 / modulus)
 
     skip = lax.dynamic_index_in_dim(skip_weight, chan, keepdims=False)
-    mixed = (conv + skip * x_rows).reshape(seq_parts * length)
+    mixed = conv + skip * x_rows
     tap_count = short_taps.shape[0]
     taps = lax.dynamic_index_in_dim(short_taps, chan, axis=1, keepdims=False)
-    padded = jnp.concatenate([jnp.zeros((tap_count - 1,), mixed.dtype), mixed])
-    total = seq_parts * length
-    short = jnp.zeros_like(mixed)
+    rim = tap_count - 1
+    tails = jnp.concatenate([jnp.zeros((1, rim), mixed.dtype), mixed[:-1, length - rim :]], 0)
+    extended = jnp.concatenate([tails, mixed], 1)
+    window = lax.dynamic_slice_in_dim(extended, half * piece, piece + rim, axis=1)
+    back = jnp.zeros((seq_parts, piece), mixed.dtype)
     for offset in range(tap_count):
-        start = tap_count - 1 - offset
-        short = short + taps[offset] * padded[start : start + total]
-    short_rows = short.reshape(seq_parts, length)
-    back = lax.dynamic_slice_in_dim(short_rows, half * piece, piece, axis=1)
+        start = rim - offset
+        back = back + taps[offset] * window[:, start : start + piece]
     got = lax.all_to_all(back, "seq", 0, 0, tiled=True)
     short_local = got.reshape(width, length)
 

time: 96 us -> 95.7 us (level)
    add x1, other arithmetic: 0.04 us -> 4.6 us  [local(): back = back + taps[offset] * window[:, start:start + piece]]
    mul x1 -> x0, other arithmetic: 4.02 us -> none  [local(): short = short + taps[offset] * padded[start:start + total]]
where the time goes in v2:
time: 95.7 us; the launch traced here: 95 us
  blocking collectives  34.7 us (36%)
  starting transfers between devices  23 us (24%)
  waiting for transfers between devices  18 us (19%)
  other arithmetic  9.15 us (10%)
  matrix products  5.56 us (6%)
  local copies, waits for them, and re-layouts  4.32 us (5%)
    all_to_all x1, blocking collectives, local(): got = lax.all_to_all(back, 'seq', 0, 0, tiled=True)  26.3 us
    all_to_all x1, starting transfers between devices, local(): recv = lax.all_to_all(send, 'seq', 0, 0, tiled=True)  23 us
    all_to_all x1, waiting for transfers between devices, local(): recv = lax.all_to_all(send, 'seq', 0, 0, tiled=True)  18 us
    psum x1, blocking collectives, local(): energy = lax.psum(jnp.sum(short_local * short_local, 0), 'ch')  8.44 us
    dot_general x18, matrix products, mat(): return jnp.dot(a, b, precision=highest, preferred_element_type=jnp.float32)  5.56 us
    add x1, other arithmetic, local(): back = back + taps[offset] * window[:, start:start + piece]  4.6 us
    sin x2, other arithmetic, phases(): return (jnp.cos(angles), direction * jnp.sin(angles))  2.07 us
  transfers between devices with their start and end apart: 1, of which 1 were waited for; matrix products, arithmetic and copies ran while one was open for 4% of the time, Pallas kernels for 0%

profile of v2, /device:TPU:1, one launch (start us, length us, event | category | flops | bytes accessed | tf_op | source)
XLA Modules:
  0.0 95.0 jit_solution(2177508222921983447)
XLA Ops:
  0.0 0.8 bitcast_convert_fusion
  1.0 0.8 broadcast_in_dim.2
  1.8 23.0 %all-to-all-start = ((f32[128,2,256]{2,1,0:T(2,128)}), f32[128,2,256]{2,1,0:T(2,128)S(1)}, u32[]{:S(2)}, u32[]{:S(2)}) async-start(f32[128,2,256]{2,1,0:T(2,128)} %bitcast.3), calls=%async_computation | async-start | bytes 524288 | tf_op jit(solution)/shard_map/all_to_all | solution.py:45
  24.8 1.0 %fusion.36 = (f32[256,256]{1,0:T(8,128)S(1)}, f32[256,256]{1,0:T(8,128)S(1)}) fusion(), kind=kLoop, calls=%fused_computation.61 | loop fusion | flops 917504 | bytes 524288 | tf_op jit(solution)/shard_map/sin | solution.py:14
  25.9 1.0 %fusion.34 = (f32[256,256]{1,0:T(8,128)S(1)}, f32[256,256]{1,0:T(8,128)S(1)}) fusion(), kind=kLoop, calls=%fused_computation.59 | loop fusion | flops 917504 | bytes 524288 | tf_op jit(solution)/shard_map/sin | solution.py:14
  26.9 0.6 copy-done.3
  27.6 0.6 dynamic_slice.12
  28.2 0.6 fusion.51
  28.8 18.0 %all-to-all-done = f32[128,2,256]{2,1,0:T(2,128)S(1)} async-done(((f32[128,2,256]{2,1,0:T(2,128)}), f32[128,2,256]{2,1,0:T(2,128)S(1)}, u32[]{:S(2)}, u32[]{:S(2)}) %all-to-all-start) | async-done | bytes 262176 | tf_op jit(solution)/shard_map/all_to_all | solution.py:45
  47.6 0.3 fusion.43
  47.9 0.3 multiply_add_fusion.1
  48.2 0.3 fusion.20
  48.5 0.3 fusion.53
  48.7 0.3 fusion.22
  49.0 0.3 fusion.52
  49.3 0.3 convolution_subtract_fusion.1
  49.6 0.3 convolution_add_fusion.1
  49.9 0.3 convolution_subtract_fusion.2
  50.2 0.3 multiply_add_fusion
  50.5 0.3 fusion.55
  50.8 0.3 fusion.54
  51.1 0.3 convolution_add_fusion
  51.3 0.3 convolution_subtract_fusion
  51.6 0.3 fusion.9
  51.9 0.9 fusion.1
  53.0 4.6 %fusion.44 = f32[128,128]{1,0:T(8,128)S(1)} fusion(f32[128,134]{1,0:T(8,128)S(1)} %fusion.26, f32[]{:T(128)} %bitcast.11, f32[]{:T(128)} %bitcast.10, f32[]{:T(128)} %bitcast.9, f32[]{:T(128)} %bitcast.8, f32[]{:T(128)} %bitcast.7, f32[]{:T(128)} %bitcast.6, f32[]{:T(128)} %bitcast), kind=kLoop, calls=%fused_computation.70 | loop fusion | flops 212992 | bytes 524316 | tf_op jit(solution)/shard_map/add | solution.py:86
  57.6 26.3 %all_to_all.14 = f32[128,1,128]{2,1,0:T(1,128)S(1)} all-to-all(f32[128,1,128]{2,1,0:T(1,128)S(1)} %bitcast.49), channel_id=1, replica_groups=mesh['seq'=128,'ch'=4] {'seq'}, dimensions={0} | all-to-all | bytes 131072 | tf_op jit(solution)/shard_map/all_to_all | solution.py:87
  83.9 0.5 broadcast.39
  84.4 0.8 reduce.3
  85.2 8.4 %psum.7 = f32[256]{0:T(256)S(1)} all-reduce(f32[256]{0:T(256)S(1)} %multiply_reduce_fusion), channel_id=1, replica_groups=mesh['seq'=128,'ch'=4] {'ch'}, use_global_device_ids=true, to_apply=%region_1.2 | all-reduce | flops 256 | bytes 2048 | tf_op jit(solution)/shard_map/psum | solution.py:90
  93.7 0.6 copy-done.2
  94.3 0.7 multiply_multiply_fusion
  (17 shorter events, 1.2 us)
Async XLA Ops:
  0.0 28.1 %copy-start = (f32[7,64]{1,0:T(8,128)S(1)}, f32[7,64]{1,0:T(8,128)}, u32[]{:S(2)}) copy-start(f32[7,64]{1,0:T(8,128)} %param.8) | copy-start | bytes 5380
  0.0 0.9 copy-start.1
  1.8 45.1 %all-to-all-start = ((f32[128,2,256]{2,1,0:T(2,128)}), f32[128,2,256]{2,1,0:T(2,128)S(1)}, u32[]{:S(2)}, u32[]{:S(2)}) async-start(f32[128,2,256]{2,1,0:T(2,128)} %bitcast.3), calls=%async_computation | async-start | bytes 524288 | tf_op jit(solution)/shard_map/all_to_all | solution.py:45
  26.9 0.7 copy-start.3
  93.7 0.7 copy-start.2

commit v3 on v2

--- a/solution.py
+++ b/solution.py
@@ -76,14 +76,15 @@
     mixed = conv + skip * x_rows
     tap_count = short_taps.shape[0]
     taps = lax.dynamic_index_in_dim(short_taps, chan, axis=1, keepdims=False)
-    rim = tap_count - 1
-    tails = jnp.concatenate([jnp.zeros((1, rim), mixed.dtype), mixed[:-1, length - rim :]], 0)
-    extended = jnp.concatenate([tails, mixed], 1)
-    window = lax.dynamic_slice_in_dim(extended, half * piece, piece + rim, axis=1)
-    back = jnp.zeros((seq_parts, piece), mixed.dtype)
+    earlier = jnp.concatenate([jnp.zeros((1, length), mixed.dtype), mixed[:-1]], 0)
+    joined = jnp.concatenate([mixed, earlier], 1)
+    source = jnp.arange(2 * length, dtype=jnp.int32)
+    source = jnp.where(source < length, source, source - 2 * length)
+    lag = (half * piece + jnp.arange(piece, dtype=jnp.int32))[None, :] - source[:, None]
+    band = jnp.zeros(lag.shape, mixed.dtype)
     for offset in range(tap_count):
-        start = rim - offset
-        back = back + taps[offset] * window[:, start : start + piece]
+        band = band + jnp.where(lag == offset, taps[offset], 0.0)
+    back = mat(joined, band)
     got = lax.all_to_all(back, "seq", 0, 0, tiled=True)
     short_local = got.reshape(width, length)
 

time: 95.7 us -> 95.8 us (level)
  matrix products: 5.56 us -> 10.5 us
  other arithmetic: 9.15 us -> 4.43 us
    dot_general x18 -> x19, matrix products: 5.56 us -> 10.5 us  [mat(): return jnp.dot(a, b, precision=highest, preferred_element_type=jnp.float32)]
    add x1, other arithmetic: 4.6 us -> 0.01 us  [local(): half * piece + jnp.arange(piece, dtype=jnp.int32)]
where the time goes in v3:
time: 95.8 us; the launch traced here: 95.2 us
  blocking collectives  34.7 us (36%)
  starting transfers between devices  23 us (24%)
  waiting for transfers between devices  18 us (19%)
  matrix products  10.5 us (11%)
  other arithmetic  4.43 us (5%)
  local copies, waits for them, and re-layouts  4.25 us (4%)
    all_to_all x1, blocking collectives, local(): got = lax.all_to_all(back, 'seq', 0, 0, tiled=True)  26.3 us
    all_to_all x1, starting transfers between devices, local(): recv = lax.all_to_all(send, 'seq', 0, 0, tiled=True)  23 us
    all_to_all x1, waiting for transfers between devices, local(): recv = lax.all_to_all(send, 'seq', 0, 0, tiled=True)  18 us
    dot_general x19, matrix products, mat(): return jnp.dot(a, b, precision=highest, preferred_element_type=jnp.float32)  10.5 us
    psum x1, blocking collectives, local(): energy = lax.psum(jnp.sum(short_local * short_local, 0), 'ch')  8.44 us
    sin x2, other arithmetic, phases(): return (jnp.cos(angles), direction * jnp.sin(angles))  2.07 us
  transfers between devices with their start and end apart: 1, of which 1 were waited for; matrix products, arithmetic and copies ran while one was open for 4% of the time, Pallas kernels for 0%

profile of v3, /device:TPU:1, one launch (start us, length us, event | category | flops | bytes accessed | tf_op | source)
XLA Modules:
  0.0 95.2 jit_solution(6051591579889972655)
XLA Ops:
  0.0 0.8 bitcast_convert_fusion
  1.0 0.8 broadcast_in_dim.44
  1.8 23.0 %all-to-all-start = ((f32[128,2,256]{2,1,0:T(2,128)}), f32[128,2,256]{2,1,0:T(2,128)S(1)}, u32[]{:S(2)}, u32[]{:S(2)}) async-start(f32[128,2,256]{2,1,0:T(2,128)} %bitcast.2), calls=%async_computation | async-start | bytes 524288 | tf_op jit(solution)/shard_map/all_to_all | solution.py:45
  24.8 1.0 %fusion.69 = (f32[256,256]{1,0:T(8,128)S(1)}, f32[256,256]{1,0:T(8,128)S(1)}) fusion(), kind=kLoop, calls=%fused_computation.100 | loop fusion | flops 917504 | bytes 524288 | tf_op jit(solution)/shard_map/sin | solution.py:14
  25.8 1.0 %fusion.67 = (f32[256,256]{1,0:T(8,128)S(1)}, f32[256,256]{1,0:T(8,128)S(1)}) fusion(), kind=kLoop, calls=%fused_computation.98 | loop fusion | flops 917504 | bytes 524288 | tf_op jit(solution)/shard_map/sin | solution.py:14
  26.9 0.6 copy-done.3
  27.6 0.6 dynamic_slice.8
  28.2 0.6 fusion.88
  28.8 18.0 %all-to-all-done = f32[128,2,256]{2,1,0:T(2,128)S(1)} async-done(((f32[128,2,256]{2,1,0:T(2,128)}), f32[128,2,256]{2,1,0:T(2,128)S(1)}, u32[]{:S(2)}, u32[]{:S(2)}) %all-to-all-start) | async-done | bytes 262176 | tf_op jit(solution)/shard_map/all_to_all | solution.py:45
  47.6 0.3 fusion.76
  47.9 0.3 multiply_add_fusion.1
  48.2 0.3 fusion.36
  48.5 0.3 fusion.90
  48.7 0.3 fusion.38
  49.0 0.3 fusion.89
  49.3 0.3 convolution_subtract_fusion.1
  49.6 0.3 convolution_add_fusion.1
  49.9 0.3 convolution_subtract_fusion.2
  50.2 0.3 multiply_add_fusion
  50.5 0.3 fusion.92
  50.8 0.3 fusion.91
  51.1 0.3 convolution_add_fusion
  51.3 0.3 convolution_subtract_fusion
  51.6 0.3 fusion.25
  51.9 0.9 fusion.1
  52.8 4.9 %fusion.6 = f32[128,128]{1,0:T(8,128)S(1)} fusion(f32[127,256]{1,0:T(8,128)S(1)} %bitcast.50, f32[128,256]{1,0:T(8,128)S(1)} %fusion.1, f32[]{:T(128)} %bitcast.11, f32[]{:T(128)} %bitcast.10, f32[]{:T(128)} %bitcast.9, f32[]{:T(128)} %bitcast.8, f32[]{:T(128)} %bitcast.7, f32[]{:T(128)} %bitcast.6, f32[]{:T(128)} %bitcast.5, ...), kind=kOutput, calls=%fused_computation.26 | convolution fusion | flops 51904512 | bytes 329244 | tf_op jit(solution)/shard_map/dot_general | solution.py:18
  57.7 26.3 %all_to_all.14 = f32[128,1,128]{2,1,0:T(1,128)S(1)} all-to-all(f32[128,1,128]{2,1,0:T(1,128)S(1)} %bitcast.51), channel_id=1, replica_groups=mesh['seq'=128,'ch'=4] {'seq'}, dimensions={0} | all-to-all | bytes 131072 | tf_op jit(solution)/shard_map/all_to_all | solution.py:88
  84.0 0.5 broadcast.57
  84.5 0.8 reduce.3
  85.4 8.4 %psum.7 = f32[256]{0:T(256)S(1)} all-reduce(f32[256]{0:T(256)S(1)} %multiply_reduce_fusion), channel_id=1, replica_groups=mesh['seq'=128,'ch'=4] {'ch'}, use_global_device_ids=true, to_apply=%region_1.2 | all-reduce | flops 256 | bytes 2048 | tf_op jit(solution)/shard_map/psum | solution.py:91
  93.8 0.6 copy-done.2
  94.5 0.7 multiply_multiply_fusion
  (17 shorter events, 1.0 us)
Async XLA Ops:
  0.0 28.1 %copy-start = (f32[7,64]{1,0:T(8,128)S(1)}, f32[7,64]{1,0:T(8,128)}, u32[]{:S(2)}) copy-start(f32[7,64]{1,0:T(8,128)} %param.8) | copy-start | bytes 5380
  0.0 0.9 copy-start.1
  1.8 45.1 %all-to-all-start = ((f32[128,2,256]{2,1,0:T(2,128)}), f32[128,2,256]{2,1,0:T(2,128)S(1)}, u32[]{:S(2)}, u32[]{:S(2)}) async-start(f32[128,2,256]{2,1,0:T(2,128)} %bitcast.2), calls=%async_computation | async-start | bytes 524288 | tf_op jit(solution)/shard_map/all_to_all | solution.py:45
  26.9 0.7 copy-start.3
  93.8 0.7 copy-start.2

commit v4 on v3

--- a/solution.py
+++ b/solution.py
@@ -84,6 +84,7 @@
     band = jnp.zeros(lag.shape, mixed.dtype)
     for offset in range(tap_count):
         band = band + jnp.where(lag == offset, taps[offset], 0.0)
+    band = lax.optimization_barrier(band)
     back = mat(joined, band)
     got = lax.all_to_all(back, "seq", 0, 0, tiled=True)
     short_local = got.reshape(width, length)

time: 95.8 us -> 91.1 us (0.951)
  waiting for transfers between devices: 18 us -> 13.3 us
  other arithmetic: 4.43 us -> 9.06 us
  matrix products: 10.5 us -> 5.87 us
    all_to_all x1, waiting for transfers between devices: 18 us -> 13.3 us  [local(): recv = lax.all_to_all(send, 'seq', 0, 0, tiled=True)]
    dot_general x19, matrix products: 10.5 us -> 5.87 us  [mat(): return jnp.dot(a, b, precision=highest, preferred_element_type=jnp.float32)]
    add x0 -> x1, other arithmetic: none -> 4.63 us  [local(): band = band + jnp.where(lag == offset, taps[offset], 0.0)]
  transfers between devices with their start and end apart: 1 -> 1, of which waited for: 1 -> 1; matrix products, arithmetic and copies ran while one was open for 4% -> 9% of each run, Pallas kernels for 0% -> 0%
where the time goes in v4:
time: 91.1 us; the launch traced here: 90.5 us
  blocking collectives  34.7 us (38%)
  starting transfers between devices  23 us (25%)
  waiting for transfers between devices  13.3 us (15%)
  other arithmetic  9.06 us (10%)
  matrix products  5.87 us (6%)
  local copies, waits for them, and re-layouts  4.33 us (5%)
    all_to_all x1, blocking collectives, local(): got = lax.all_to_all(back, 'seq', 0, 0, tiled=True)  26.3 us
    all_to_all x1, starting transfers between devices, local(): recv = lax.all_to_all(send, 'seq', 0, 0, tiled=True)  23 us
    all_to_all x1, waiting for transfers between devices, local(): recv = lax.all_to_all(send, 'seq', 0, 0, tiled=True)  13.3 us
    psum x1, blocking collectives, local(): energy = lax.psum(jnp.sum(short_local * short_local, 0), 'ch')  8.44 us
    dot_general x19, matrix products, mat(): return jnp.dot(a, b, precision=highest, preferred_element_type=jnp.float32)  5.87 us
    add x1, other arithmetic, local(): band = band + jnp.where(lag == offset, taps[offset], 0.0)  4.63 us
    sin x2, other arithmetic, phases(): return (jnp.cos(angles), direction * jnp.sin(angles))  2.07 us
  transfers between devices with their start and end apart: 1, of which 1 were waited for; matrix products, arithmetic and copies ran while one was open for 9% of the time, Pallas kernels for 0%

profile of v4, /device:TPU:1, one launch (start us, length us, event | category | flops | bytes accessed | tf_op | source)
XLA Modules:
  0.0 90.5 jit_solution(14773382815954833466)
XLA Ops:
  0.0 0.8 bitcast_convert_fusion
  1.0 0.8 broadcast_in_dim.44
  1.8 23.0 %all-to-all-start = ((f32[128,2,256]{2,1,0:T(2,128)}), f32[128,2,256]{2,1,0:T(2,128)S(1)}, u32[]{:S(2)}, u32[]{:S(2)}) async-start(f32[128,2,256]{2,1,0:T(2,128)} %bitcast.2), calls=%async_computation | async-start | bytes 524288 | tf_op jit(solution)/shard_map/all_to_all | solution.py:45
  24.8 1.0 %fusion.37 = (f32[256,256]{1,0:T(8,128)S(1)}, f32[256,256]{1,0:T(8,128)S(1)}) fusion(), kind=kLoop, calls=%fused_computation.69 | loop fusion | flops 917504 | bytes 524288 | tf_op jit(solution)/shard_map/sin | solution.py:14
  25.8 1.0 %fusion.39 = (f32[256,256]{1,0:T(8,128)S(1)}, f32[256,256]{1,0:T(8,128)S(1)}) fusion(), kind=kLoop, calls=%fused_computation.71 | loop fusion | flops 917504 | bytes 524288 | tf_op jit(solution)/shard_map/sin | solution.py:14
  26.9 0.6 copy-done.3
  27.6 0.7 dynamic_slice.8
  28.3 0.6 fusion.51
  28.9 4.6 %select_add_fusion = f32[512,128]{1,0:T(8,128)S(1)} fusion(f32[]{:T(128)} %bitcast.11, f32[]{:T(128)} %bitcast.10, f32[]{:T(128)} %bitcast.9, f32[]{:T(128)} %bitcast.8, f32[]{:T(128)} %bitcast.7, f32[]{:T(128)} %bitcast.6, f32[]{:T(128)} %bitcast.5, s32[512]{0:T(512)S(1)} %compare_select_fusion, s32[128]{0:T(128)S(1)} %iota_add_fusion), kind=kLoop, calls=%fused_computation.30 | loop fusion | flops 1376256 | bytes 264732 | tf_op jit(solution)/shard_map/add | solution.py:86
  33.6 13.3 %all-to-all-done = f32[128,2,256]{2,1,0:T(2,128)S(1)} async-done(((f32[128,2,256]{2,1,0:T(2,128)}), f32[128,2,256]{2,1,0:T(2,128)S(1)}, u32[]{:S(2)}, u32[]{:S(2)}) %all-to-all-start) | async-done | bytes 262176 | tf_op jit(solution)/shard_map/all_to_all | solution.py:45
  47.9 0.3 multiply_add_fusion.1
  48.2 0.3 fusion.23
  48.5 0.3 fusion.53
  48.7 0.3 fusion.52
  49.0 0.3 fusion.25
  49.3 0.3 convolution_add_fusion.1
  49.6 0.3 convolution_subtract_fusion.1
  49.9 0.3 convolution_subtract_fusion.2
  50.2 0.3 multiply_add_fusion
  50.5 0.3 fusion.54
  50.8 0.3 fusion.55
  51.1 0.3 convolution_subtract_fusion
  51.3 0.3 convolution_add_fusion
  51.6 0.3 fusion.12
  51.9 0.9 %fusion.1 = f32[128,256]{1,0:T(8,128)S(1)} fusion(f32[128,256]{1,0:T(8,128)S(1)} %fusion.12, f32[256,256]{1,0:T(8,128)S(1)} %convolution_add_fusion, f32[256,256]{1,0:T(8,128)S(1)} %get-tuple-element.10, f32[256,256]{1,0:T(8,128)S(1)} %convolution_subtract_fusion, f32[256,256]{1,0:T(8,128)S(1)} %get-tuple-element.12, f32[256,256]{1,0:T(8,128)S(1)} %get-tuple-element.11, ...), kind=kOutput, calls=%fused_computation.8 | convolution fusion | flops 50659328 | bytes 1572868 | tf_op jit(solution)/shard_map/dot_general | solution.py:18
  52.8 0.3 fusion.6
  53.1 26.3 %all_to_all.14 = f32[128,1,128]{2,1,0:T(1,128)S(1)} all-to-all(f32[128,1,128]{2,1,0:T(1,128)S(1)} %bitcast.52), channel_id=1, replica_groups=mesh['seq'=128,'ch'=4] {'seq'}, dimensions={0} | all-to-all | bytes 131072 | tf_op jit(solution)/shard_map/all_to_all | solution.py:89
  79.4 0.5 broadcast.57
  79.9 0.8 reduce.3
  80.7 8.4 %psum.7 = f32[256]{0:T(256)S(1)} all-reduce(f32[256]{0:T(256)S(1)} %multiply_reduce_fusion), channel_id=1, replica_groups=mesh['seq'=128,'ch'=4] {'ch'}, use_global_device_ids=true, to_apply=%region_1.2 | all-reduce | flops 256 | bytes 2048 | tf_op jit(solution)/shard_map/psum | solution.py:92
  89.2 0.6 copy-done.2
  89.8 0.7 multiply_multiply_fusion
  (18 shorter events, 1.3 us)
Async XLA Ops:
  0.0 28.2 %copy-start = (f32[7,64]{1,0:T(8,128)S(1)}, f32[7,64]{1,0:T(8,128)}, u32[]{:S(2)}) copy-start(f32[7,64]{1,0:T(8,128)} %param.8) | copy-start | bytes 5380
  0.0 0.9 copy-start.1
  1.8 45.1 %all-to-all-start = ((f32[128,2,256]{2,1,0:T(2,128)}), f32[128,2,256]{2,1,0:T(2,128)S(1)}, u32[]{:S(2)}, u32[]{:S(2)}) async-start(f32[128,2,256]{2,1,0:T(2,128)} %bitcast.2), calls=%async_computation | async-start | bytes 524288 | tf_op jit(solution)/shard_map/all_to_all | solution.py:45
  26.9 0.7 copy-start.3
  89.2 0.7 copy-start.2

commit v5 on v4

--- a/solution.py
+++ b/solution.py
@@ -89,8 +89,11 @@
     got = lax.all_to_all(back, "seq", 0, 0, tiled=True)
     short_local = got.reshape(width, length)
 
-    energy = lax.psum(jnp.sum(short_local * short_local, 0), "ch")
-    all_channels = width * lax.axis_size("ch")
+    groups = lax.axis_size("ch")
+    partial = jnp.sum(short_local * short_local, 0)
+    spread = jnp.broadcast_to(partial[None], (groups,) + partial.shape)
+    energy = jnp.sum(lax.all_to_all(spread, "ch", 0, 0, tiled=True), 0)
+    all_channels = width * groups
     return short_local * norm_gain[:, None] * lax.rsqrt(energy / all_channels + 1e-06)[None, :]
 
 

time: 91.1 us -> 90.3 us (level)
    psum x1 -> x0, blocking collectives: 8.44 us -> none  [local(): energy = lax.psum(jnp.sum(short_local * short_local, 0), 'ch')]
    all_to_all x0 -> x1, blocking collectives: none -> 7.81 us  [local(): energy = jnp.sum(lax.all_to_all(spread, 'ch', 0, 0, tiled=True), 0)]
where the time goes in v5:
time: 90.3 us; the launch traced here: 89.9 us
  blocking collectives  34.1 us (38%)
  starting transfers between devices  23 us (25%)
  waiting for transfers between devices  13.3 us (15%)
  other arithmetic  9.08 us (10%)
  matrix products  5.87 us (7%)
  local copies, waits for them, and re-layouts  4.32 us (5%)
    all_to_all x1, blocking collectives, local(): got = lax.all_to_all(back, 'seq', 0, 0, tiled=True)  26.3 us
    all_to_all x1, starting transfers between devices, local(): recv = lax.all_to_all(send, 'seq', 0, 0, tiled=True)  23 us
    all_to_all x1, waiting for transfers between devices, local(): recv = lax.all_to_all(send, 'seq', 0, 0, tiled=True)  13.3 us
    all_to_all x1, blocking collectives, local(): energy = jnp.sum(lax.all_to_all(spread, 'ch', 0, 0, tiled=True), 0)  7.81 us
    dot_general x19, matrix products, mat(): return jnp.dot(a, b, precision=highest, preferred_element_type=jnp.float32)  5.87 us
    add x1, other arithmetic, local(): band = band + jnp.where(lag == offset, taps[offset], 0.0)  4.63 us
    sin x2, other arithmetic, phases(): return (jnp.cos(angles), direction * jnp.sin(angles))  2.07 us
  transfers between devices with their start and end apart: 1, of which 1 were waited for; matrix products, arithmetic and copies ran while one was open for 9% of the time, Pallas kernels for 0%

profile of v5, /device:TPU:1, one launch (start us, length us, event | category | flops | bytes accessed | tf_op | source)
XLA Modules:
  0.0 89.9 jit_solution(5724486599435697639)
XLA Ops:
  0.0 0.8 bitcast_convert_fusion
  1.0 0.8 broadcast_in_dim.50
  1.8 23.0 %all-to-all-start = ((f32[128,2,256]{2,1,0:T(2,128)}), f32[128,2,256]{2,1,0:T(2,128)S(1)}, u32[]{:S(2)}, u32[]{:S(2)}) async-start(f32[128,2,256]{2,1,0:T(2,128)} %bitcast.2), calls=%async_computation | async-start | bytes 524288 | tf_op jit(solution)/shard_map/all_to_all | solution.py:45
  24.8 1.0 %fusion.37 = (f32[256,256]{1,0:T(8,128)S(1)}, f32[256,256]{1,0:T(8,128)S(1)}) fusion(), kind=kLoop, calls=%fused_computation.69 | loop fusion | flops 917504 | bytes 524288 | tf_op jit(solution)/shard_map/sin | solution.py:14
  25.8 1.0 %fusion.39 = (f32[256,256]{1,0:T(8,128)S(1)}, f32[256,256]{1,0:T(8,128)S(1)}) fusion(), kind=kLoop, calls=%fused_computation.71 | loop fusion | flops 917504 | bytes 524288 | tf_op jit(solution)/shard_map/sin | solution.py:14
  26.9 0.6 copy-done.3
  27.6 0.7 dynamic_slice.8
  28.3 0.6 fusion.51
  28.9 4.6 %select_add_fusion = f32[512,128]{1,0:T(8,128)S(1)} fusion(f32[]{:T(128)} %bitcast.11, f32[]{:T(128)} %bitcast.10, f32[]{:T(128)} %bitcast.9, f32[]{:T(128)} %bitcast.8, f32[]{:T(128)} %bitcast.7, f32[]{:T(128)} %bitcast.6, f32[]{:T(128)} %bitcast.5, s32[512]{0:T(512)S(1)} %compare_select_fusion, s32[128]{0:T(128)S(1)} %iota_add_fusion), kind=kLoop, calls=%fused_computation.30 | loop fusion | flops 1376256 | bytes 264732 | tf_op jit(solution)/shard_map/add | solution.py:86
  33.6 13.3 %all-to-all-done = f32[128,2,256]{2,1,0:T(2,128)S(1)} async-done(((f32[128,2,256]{2,1,0:T(2,128)}), f32[128,2,256]{2,1,0:T(2,128)S(1)}, u32[]{:S(2)}, u32[]{:S(2)}) %all-to-all-start) | async-done | bytes 262176 | tf_op jit(solution)/shard_map/all_to_all | solution.py:45
  47.9 0.3 multiply_add_fusion.1
  48.2 0.3 fusion.23
  48.5 0.3 fusion.53
  48.7 0.3 fusion.52
  49.0 0.3 fusion.25
  49.3 0.3 convolution_add_fusion.1
  49.6 0.3 convolution_subtract_fusion.1
  49.9 0.3 convolution_subtract_fusion.2
  50.2 0.3 multiply_add_fusion
  50.5 0.3 fusion.54
  50.8 0.3 fusion.55
  51.1 0.3 convolution_subtract_fusion
  51.3 0.3 convolution_add_fusion
  51.6 0.3 fusion.12
  51.9 0.9 %fusion.1 = f32[128,256]{1,0:T(8,128)S(1)} fusion(f32[128,256]{1,0:T(8,128)S(1)} %fusion.12, f32[256,256]{1,0:T(8,128)S(1)} %convolution_add_fusion, f32[256,256]{1,0:T(8,128)S(1)} %get-tuple-element.10, f32[256,256]{1,0:T(8,128)S(1)} %convolution_subtract_fusion, f32[256,256]{1,0:T(8,128)S(1)} %get-tuple-element.12, f32[256,256]{1,0:T(8,128)S(1)} %get-tuple-element.11, ...), kind=kOutput, calls=%fused_computation.8 | convolution fusion | flops 50659328 | bytes 1572868 | tf_op jit(solution)/shard_map/dot_general | solution.py:18
  52.8 0.3 fusion.6
  53.1 26.3 %all_to_all.20 = f32[128,1,128]{2,1,0:T(1,128)S(1)} all-to-all(f32[128,1,128]{2,1,0:T(1,128)S(1)} %bitcast.52), channel_id=1, replica_groups=mesh['seq'=128,'ch'=4] {'seq'}, dimensions={0} | all-to-all | bytes 131072 | tf_op jit(solution)/shard_map/all_to_all | solution.py:89
  79.4 0.5 broadcast.67
  79.9 0.8 reduce.4
  80.7 7.8 %all_to_all.21 = f32[4,1,256]{2,1,0:T(1,128)S(1)} all-to-all(f32[4,1,256]{2,1,0:T(1,128)S(1)} %broadcast_in_dim.59), channel_id=1, replica_groups=mesh['seq'=128,'ch'=4] {'ch'}, dimensions={0} | all-to-all | bytes 8192 | tf_op jit(solution)/shard_map/all_to_all | solution.py:95
  88.6 0.6 copy-done.2
  89.2 0.7 multiply_multiply_fusion
  (20 shorter events, 1.3 us)
Async XLA Ops:
  0.0 28.2 %copy-start = (f32[7,64]{1,0:T(8,128)S(1)}, f32[7,64]{1,0:T(8,128)}, u32[]{:S(2)}) copy-start(f32[7,64]{1,0:T(8,128)} %param.8) | copy-start | bytes 5380
  0.0 0.9 copy-start.1
  1.8 45.1 %all-to-all-start = ((f32[128,2,256]{2,1,0:T(2,128)}), f32[128,2,256]{2,1,0:T(2,128)S(1)}, u32[]{:S(2)}, u32[]{:S(2)}) async-start(f32[128,2,256]{2,1,0:T(2,128)} %bitcast.2), calls=%async_computation | async-start | bytes 524288 | tf_op jit(solution)/shard_map/all_to_all | solution.py:45
  26.9 0.7 copy-start.3
  88.6 0.7 copy-start.2

commit v6 on v5

--- a/solution.py
+++ b/solution.py
@@ -41,10 +41,9 @@
     signal_f = signal.astype(jnp.float32)
 
     both = jnp.stack([signal_f, long_filter], 1)
-    send = jnp.repeat(both, dup, axis=0)
-    recv = lax.all_to_all(send, "seq", 0, 0, tiled=True)
-    x_rows = recv[:, 0, :]
-    h_rows = recv[:, 1, :]
+    mine = lax.all_to_all(both.reshape(seq_parts, length), "seq", 0, 0, tiled=True)
+    other = lax.ppermute(mine, "seq", [(i, i ^ 1) for i in range(seq_parts)])
+    x_rows = jnp.where(half == 0, mine, other)
 
     rows = 2 * seq_parts
     cols = length
@@ -65,8 +64,8 @@
         yr, yi = cmul(yr, yi, turn_fwd[0], turn_fwd[1])
         return cmat(yr, yi, cols_fwd[0], cols_fwd[1])
 
-    xr, xi = forward(x_rows)
-    hr, hi = forward(h_rows)
+    xr, xi = forward(mine)
+    hr, hi = forward(other)
     pr, pi = cmul(xr, xi, hr, hi)
     qr, qi = cmat(pr, pi, cols_inv[0], cols_inv[1])
     qr, qi = cmul(qr, qi, turn_fwd[0], -turn_fwd[1])

time: 90.3 us -> 88.5 us (0.980)
  starting transfers between devices: 23 us -> 25.6 us
  waiting for transfers between devices: 13.3 us -> 10.9 us
  blocking collectives: 34.1 us -> 32.3 us
    all_to_all x1, waiting for transfers between devices: 13.3 us -> 10.5 us  [local(): lax.all_to_all(both.reshape(seq_parts, length), 'seq', 0, 0, tiled=True)]
    ppermute x0 -> x1, starting transfers between devices: none -> 2.62 us  [local(): other = lax.ppermute(mine, 'seq', [(i, i ^ 1) for i in range(seq_parts)])]
    all_to_all x1, blocking collectives: 26.3 us -> 24.5 us  [local(): got = lax.all_to_all(back, 'seq', 0, 0, tiled=True)]
  transfers between devices with their start and end apart: 1 -> 2, of which waited for: 1 -> 2; matrix products, arithmetic and copies ran while one was open for 9% -> 10% of each run, Pallas kernels for 0% -> 0%
where the time goes in v6:
time: 88.5 us; the launch traced here: 88.1 us
  blocking collectives  32.3 us (36%)
  starting transfers between devices  25.6 us (29%)
  waiting for transfers between devices  10.9 us (12%)
  other arithmetic  8.96 us (10%)
  matrix products  5.8 us (7%)
  local copies, waits for them, and re-layouts  4.17 us (5%)
    all_to_all x1, blocking collectives, local(): got = lax.all_to_all(back, 'seq', 0, 0, tiled=True)  24.5 us
    all_to_all x1, starting transfers between devices, local(): lax.all_to_all(both.reshape(seq_parts, length), 'seq', 0, 0, tiled=True)  23 us
    all_to_all x1, waiting for transfers between devices, local(): lax.all_to_all(both.reshape(seq_parts, length), 'seq', 0, 0, tiled=True)  10.5 us
    all_to_all x1, blocking collectives, local(): energy = jnp.sum(lax.all_to_all(spread, 'ch', 0, 0, tiled=True), 0)  7.83 us
    dot_general x19, matrix products, mat(): return jnp.dot(a, b, precision=highest, preferred_element_type=jnp.float32)  5.8 us
    add x1, other arithmetic, local(): band = band + jnp.where(lag == offset, taps[offset], 0.0)  4.51 us
    ppermute x1, starting transfers between devices, local(): other = lax.ppermute(mine, 'seq', [(i, i ^ 1) for i in range(seq_parts)])  2.62 us
    sin x2, other arithmetic, phases(): return (jnp.cos(angles), direction * jnp.sin(angles))  2.07 us
  transfers between devices with their start and end apart: 2, of which 2 were waited for; matrix products, arithmetic and copies ran while one was open for 10% of the time, Pallas kernels for 0%

profile of v6, /device:TPU:1, one launch (start us, length us, event | category | flops | bytes accessed | tf_op | source)
XLA Modules:
  0.0 88.1 jit_solution(8113032193496075764)
XLA Ops:
  0.0 0.8 bitcast_convert_fusion
  1.0 0.8 all_to_all.18
  1.8 23.0 %all-to-all-start = ((f32[128,1,256]{2,1,0:T(1,128)}), f32[128,1,256]{2,1,0:T(1,128)S(1)}, u32[]{:S(2)}, u32[]{:S(2)}) async-start(f32[128,1,256]{2,1,0:T(1,128)} %all_to_all.18), calls=%async_computation | async-start | bytes 262144 | tf_op jit(solution)/shard_map/all_to_all | solution.py:44
  24.9 1.0 %fusion.36 = (f32[256,256]{1,0:T(8,128)S(1)}, f32[256,256]{1,0:T(8,128)S(1)}) fusion(), kind=kLoop, calls=%fused_computation.65 | loop fusion | flops 917504 | bytes 524288 | tf_op jit(solution)/shard_map/sin | solution.py:14
  25.9 1.0 %fusion.38 = (f32[256,256]{1,0:T(8,128)S(1)}, f32[256,256]{1,0:T(8,128)S(1)}) fusion(), kind=kLoop, calls=%fused_computation.67 | loop fusion | flops 917504 | bytes 524288 | tf_op jit(solution)/shard_map/sin | solution.py:14
  27.0 0.6 copy-done.3
  27.7 0.6 dynamic_slice.8
  28.4 0.6 fusion.49
  29.0 4.5 %select_add_fusion = f32[512,128]{1,0:T(8,128)S(1)} fusion(f32[]{:T(128)} %bitcast.9, f32[]{:T(128)} %bitcast.8, f32[]{:T(128)} %bitcast.7, f32[]{:T(128)} %bitcast.6, f32[]{:T(128)} %bitcast.5, f32[]{:T(128)} %bitcast.4, f32[]{:T(128)} %bitcast.3, s32[512]{0:T(512)S(1)} %compare_select_fusion, s32[128]{0:T(128)S(1)} %iota_add_fusion), kind=kLoop, calls=%fused_computation.29 | loop fusion | flops 1376256 | bytes 264732 | tf_op jit(solution)/shard_map/add | solution.py:85
  33.5 10.5 %all-to-all-done = f32[128,1,256]{2,1,0:T(1,128)S(1)} async-done(((f32[128,1,256]{2,1,0:T(1,128)}), f32[128,1,256]{2,1,0:T(1,128)S(1)}, u32[]{:S(2)}, u32[]{:S(2)}) %all-to-all-start) | async-done | bytes 131104 | tf_op jit(solution)/shard_map/all_to_all | solution.py:44
  44.0 2.6 %collective-permute-start = (f32[128,256]{1,0:T(8,128)S(1)}, f32[128,256]{1,0:T(8,128)S(1)}, u32[]{:S(2)}, u32[]{:S(2)}) collective-permute-start(f32[128,256]{1,0:T(8,128)S(1)} %bitcast.48), channel_id=1, source_target_pairs={{0,4},{4,0},{8,12},{12,8},{16,20},{20,16},{24,28},{28,24},{32,36},... | collective-permute-start | bytes 393224 | tf_op jit(solution)/shard_map/ppermute | solution.py:45
  47.1 0.4 collective-permute-done
  47.8 0.3 multiply_add_fusion.1
  48.1 0.3 fusion.22
  48.4 0.3 fusion.51
  48.7 0.3 fusion.50
  49.0 0.3 fusion.24
  49.3 0.3 convolution_add_fusion.1
  49.6 0.3 convolution_subtract_fusion.1
  49.9 0.3 convolution_subtract_fusion.2
  50.2 0.3 multiply_add_fusion
  50.5 0.3 fusion.52
  50.8 0.3 fusion.53
  51.0 0.3 convolution_subtract_fusion
  51.3 0.3 convolution_add_fusion
  51.9 0.9 multiply_add_fusion.3
  53.0 24.5 %all_to_all.27 = f32[128,1,128]{2,1,0:T(1,128)S(1)} all-to-all(f32[128,1,128]{2,1,0:T(1,128)S(1)} %bitcast.47), channel_id=1, replica_groups=mesh['seq'=128,'ch'=4] {'seq'}, dimensions={0} | all-to-all | bytes 131072 | tf_op jit(solution)/shard_map/all_to_all | solution.py:88
  77.5 0.5 broadcast.67
  78.0 0.8 reduce.4
  78.9 7.8 %all_to_all.28 = f32[4,1,256]{2,1,0:T(1,128)S(1)} all-to-all(f32[4,1,256]{2,1,0:T(1,128)S(1)} %broadcast_in_dim.55), channel_id=1, replica_groups=mesh['seq'=128,'ch'=4] {'ch'}, dimensions={0} | all-to-all | bytes 8192 | tf_op jit(solution)/shard_map/all_to_all | solution.py:94
  86.8 0.6 copy-done.2
  87.4 0.7 multiply_multiply_fusion
  (22 shorter events, 1.6 us)
Async XLA Ops:
  0.0 28.3 %copy-start = (f32[7,64]{1,0:T(8,128)S(1)}, f32[7,64]{1,0:T(8,128)}, u32[]{:S(2)}) copy-start(f32[7,64]{1,0:T(8,128)} %param.8) | copy-start | bytes 5380
  0.0 0.9 copy-start.1
  1.8 42.1 %all-to-all-start = ((f32[128,1,256]{2,1,0:T(1,128)}), f32[128,1,256]{2,1,0:T(1,128)S(1)}, u32[]{:S(2)}, u32[]{:S(2)}) async-start(f32[128,1,256]{2,1,0:T(1,128)} %all_to_all.18), calls=%async_computation | async-start | bytes 262144 | tf_op jit(solution)/shard_map/all_to_all | solution.py:44
  27.0 0.7 copy-start.3
  44.0 3.6 %collective-permute-start = (f32[128,256]{1,0:T(8,128)S(1)}, f32[128,256]{1,0:T(8,128)S(1)}, u32[]{:S(2)}, u32[]{:S(2)}) collective-permute-start(f32[128,256]{1,0:T(8,128)S(1)} %bitcast.48), channel_id=1, source_target_pairs={{0,4},{4,0},{8,12},{12,8},{16,20},{20,16},{24,28},{28,24},{32,36},... | collective-permute-start | bytes 393224 | tf_op jit(solution)/shard_map/ppermute | solution.py:45
  86.7 0.7 copy-start.2

commit v7 on v6

--- a/solution.py
+++ b/solution.py
@@ -26,6 +26,16 @@
     return (mat(ar, br) - mat(ai, bi), mat(ar, bi) + mat(ai, br))
 
 
+def gauss(ar, ai, table):
+    br, bsum, bdiff = table
+    common = mat(ar + ai, br)
+    return (common - mat(ai, bsum), common + mat(ar, bdiff))
+
+
+def with_sums(br, bi):
+    return (br, br + bi, bi - br)
+
+
 def cmul(ar, ai, br, bi):
     return (ar * br - ai * bi, ar * bi + ai * br)
 
@@ -52,22 +62,22 @@
     col_ids = jnp.arange(cols, dtype=jnp.int32)
     square = phases(col_ids, col_ids, cols, 1.0)
     turn = phases(row_ids, col_ids, modulus, 1.0)
-    square, turn = lax.optimization_barrier((square, turn))
+    cols_fwd = with_sums(square[0], -square[1])
+    cols_inv = with_sums(square[0], square[1])
+    square, turn, cols_fwd, cols_inv = lax.optimization_barrier((square, turn, cols_fwd, cols_inv))
     rows_fwd = (square[0][:, :seq_parts], -square[1][:, :seq_parts])
     turn_fwd = (turn[0], -turn[1])
-    cols_fwd = (square[0], -square[1])
-    cols_inv = square
     rows_inv = (square[0][:seq_parts], square[1][:seq_parts])
 
     def forward(x):
         yr, yi = cmat(rows_fwd[0], rows_fwd[1], x, None)
         yr, yi = cmul(yr, yi, turn_fwd[0], turn_fwd[1])
-        return cmat(yr, yi, cols_fwd[0], cols_fwd[1])
+        return gauss(yr, yi, cols_fwd)
 
     xr, xi = forward(mine)
     hr, hi = forward(other)
     pr, pi = cmul(xr, xi, hr, hi)
-    qr, qi = cmat(pr, pi, cols_inv[0], cols_inv[1])
+    qr, qi = gauss(pr, pi, cols_inv)
     qr, qi = cmul(qr, qi, turn_fwd[0], -turn_fwd[1])
     conv = (mat(rows_inv[0], qr) - mat(rows_inv[1], qi)) * (1.0 / modulus)
 

time: 88.5 us -> 89.8 us (1.015)
  other arithmetic: 8.96 us -> 11.3 us
  blocking collectives: 32.3 us -> 34.6 us
  waiting for transfers between devices: 10.9 us -> 8.65 us
  matrix products: 5.8 us -> 4.85 us
    all_to_all x1, blocking collectives: 24.5 us -> 26.8 us  [local(): got = lax.all_to_all(back, 'seq', 0, 0, tiled=True)]
    all_to_all x1, waiting for transfers between devices: 10.5 us -> 8.21 us  [local(): lax.all_to_all(both.reshape(seq_parts, length), 'seq', 0, 0, tiled=True)]
    sub x0 -> x2, other arithmetic: none -> 2.12 us  [with_sums(): return (br, br + bi, bi - br)]
    dot_general x19 -> x16, matrix products: 5.8 us -> 4.85 us  [mat(): return jnp.dot(a, b, precision=highest, preferred_element_type=jnp.float32)]
  transfers between devices with their start and end apart: 2 -> 2, of which waited for: 2 -> 2; matrix products, arithmetic and copies ran while one was open for 10% -> 12% of each run, Pallas kernels for 0% -> 0%
where the time goes in v7:
time: 89.8 us; the launch traced here: 89.4 us
  blocking collectives  34.6 us (39%)
  starting transfers between devices  25.6 us (29%)
  other arithmetic  11.3 us (13%)
  waiting for transfers between devices  8.65 us (10%)
  matrix products  4.85 us (5%)
  local copies, waits for them, and re-layouts  4.12 us (5%)
    all_to_all x1, blocking collectives, local(): got = lax.all_to_all(back, 'seq', 0, 0, tiled=True)  26.8 us
    all_to_all x1, starting transfers between devices, local(): lax.all_to_all(both.reshape(seq_parts, length), 'seq', 0, 0, tiled=True)  23 us
    all_to_all x1, waiting for transfers between devices, local(): lax.all_to_all(both.reshape(seq_parts, length), 'seq', 0, 0, tiled=True)  8.21 us
    all_to_all x1, blocking collectives, local(): energy = jnp.sum(lax.all_to_all(spread, 'ch', 0, 0, tiled=True), 0)  7.81 us
    dot_general x16, matrix products, mat(): return jnp.dot(a, b, precision=highest, preferred_element_type=jnp.float32)  4.85 us
    add x1, other arithmetic, local(): band = band + jnp.where(lag == offset, taps[offset], 0.0)  4.69 us
    ppermute x1, starting transfers between devices, local(): other = lax.ppermute(mine, 'seq', [(i, i ^ 1) for i in range(seq_parts)])  2.62 us
    sub x2, other arithmetic, with_sums(): return (br, br + bi, bi - br)  2.12 us
  transfers between devices with their start and end apart: 2, of which 2 were waited for; matrix products, arithmetic and copies ran while one was open for 12% of the time, Pallas kernels for 0%

profile of v7, /device:TPU:1, one launch (start us, length us, event | category | flops | bytes accessed | tf_op | source)
XLA Modules:
  0.0 89.4 jit_solution(18129651606180596591)
XLA Ops:
  0.0 0.8 bitcast_convert_fusion
  1.0 0.8 all_to_all.18
  1.8 23.0 %all-to-all-start = ((f32[128,1,256]{2,1,0:T(1,128)}), f32[128,1,256]{2,1,0:T(1,128)S(1)}, u32[]{:S(2)}, u32[]{:S(2)}) async-start(f32[128,1,256]{2,1,0:T(1,128)} %all_to_all.18), calls=%async_computation | async-start | bytes 262144 | tf_op jit(solution)/shard_map/all_to_all | solution.py:54
  24.9 1.1 %negate_subtract_fusion = (f32[256,256]{1,0:T(8,128)S(1)}, f32[256,256]{1,0:T(8,128)S(1)}) fusion(), kind=kLoop, calls=%fused_computation.57 | loop fusion | flops 1114112 | bytes 524288 | tf_op jit(solution)/shard_map/sub | solution.py:36
  25.9 1.0 %fusion.36 = (f32[256,256]{1,0:T(8,128)S(1)}, f32[256,256]{1,0:T(8,128)S(1)}) fusion(), kind=kLoop, calls=%fused_computation.67 | loop fusion | flops 917504 | bytes 524288 | tf_op jit(solution)/shard_map/sin | solution.py:14
  27.0 1.0 %fusion.38 = (f32[256,256]{1,0:T(8,128)S(1)}, f32[256,256]{1,0:T(8,128)S(1)}) fusion(), kind=kLoop, calls=%fused_computation.69 | loop fusion | flops 917504 | bytes 524288 | tf_op jit(solution)/shard_map/sin | solution.py:14
  28.0 1.1 %fusion.40 = (f32[256,256]{1,0:T(8,128)S(1)}, f32[256,256]{1,0:T(8,128)S(1)}) fusion(), kind=kLoop, calls=%fused_computation.71 | loop fusion | flops 1048576 | bytes 524288 | tf_op jit(solution)/shard_map/sub | solution.py:36
  29.1 0.6 copy-done.3
  29.8 0.6 dynamic_slice.8
  30.4 0.6 fusion.51
  31.1 4.7 %select_add_fusion = f32[512,128]{1,0:T(8,128)S(1)} fusion(f32[]{:T(128)} %bitcast.9, f32[]{:T(128)} %bitcast.8, f32[]{:T(128)} %bitcast.7, f32[]{:T(128)} %bitcast.6, f32[]{:T(128)} %bitcast.5, f32[]{:T(128)} %bitcast.4, f32[]{:T(128)} %bitcast.3, s32[512]{0:T(512)S(1)} %compare_select_fusion, s32[128]{0:T(128)S(1)} %iota_add_fusion), kind=kLoop, calls=%fused_computation.29 | loop fusion | flops 1376256 | bytes 264732 | tf_op jit(solution)/shard_map/add | solution.py:95
  35.8 8.2 %all-to-all-done = f32[128,1,256]{2,1,0:T(1,128)S(1)} async-done(((f32[128,1,256]{2,1,0:T(1,128)}), f32[128,1,256]{2,1,0:T(1,128)S(1)}, u32[]{:S(2)}, u32[]{:S(2)}) %all-to-all-start) | async-done | bytes 131104 | tf_op jit(solution)/shard_map/all_to_all | solution.py:54
  44.0 2.6 %collective-permute-start = (f32[128,256]{1,0:T(8,128)S(1)}, f32[128,256]{1,0:T(8,128)S(1)}, u32[]{:S(2)}, u32[]{:S(2)}) collective-permute-start(f32[128,256]{1,0:T(8,128)S(1)} %bitcast.43), channel_id=1, source_target_pairs={{0,4},{4,0},{8,12},{12,8},{16,20},{20,16},{24,28},{28,24},{32,36},... | collective-permute-start | bytes 393224 | tf_op jit(solution)/shard_map/ppermute | solution.py:55
  47.1 0.4 collective-permute-done
  47.8 0.3 multiply_add_fusion.1
  48.1 0.3 fusion.17
  48.4 0.3 convolution_add_fusion.1
  48.7 0.3 convolution_subtract_fusion.1
  49.0 0.3 fusion.19
  49.3 0.3 convolution_subtract_fusion.2
  49.5 0.3 multiply_add_fusion
  49.8 0.3 fusion.15
  50.1 0.3 convolution_subtract_fusion
  50.4 0.3 convolution_add_fusion
  50.9 0.8 multiply_add_fusion.3
  51.8 0.3 fusion.5
  52.0 26.8 %all_to_all.27 = f32[128,1,128]{2,1,0:T(1,128)S(1)} all-to-all(f32[128,1,128]{2,1,0:T(1,128)S(1)} %bitcast.42), channel_id=1, replica_groups=mesh['seq'=128,'ch'=4] {'seq'}, dimensions={0} | all-to-all | bytes 131072 | tf_op jit(solution)/shard_map/all_to_all | solution.py:98
  78.8 0.5 broadcast.83
  79.3 0.8 reduce.4
  80.2 7.8 %all_to_all.28 = f32[4,1,256]{2,1,0:T(1,128)S(1)} all-to-all(f32[4,1,256]{2,1,0:T(1,128)S(1)} %broadcast_in_dim.55), channel_id=1, replica_groups=mesh['seq'=128,'ch'=4] {'ch'}, dimensions={0} | all-to-all | bytes 8192 | tf_op jit(solution)/shard_map/all_to_all | solution.py:104
  88.1 0.6 copy-done.2
  88.7 0.7 multiply_multiply_fusion
  (21 shorter events, 1.4 us)
Async XLA Ops:
  0.0 30.4 %copy-start = (f32[7,64]{1,0:T(8,128)S(1)}, f32[7,64]{1,0:T(8,128)}, u32[]{:S(2)}) copy-start(f32[7,64]{1,0:T(8,128)} %param.8) | copy-start | bytes 5380
  0.0 0.9 copy-start.1
  1.8 42.1 %all-to-all-start = ((f32[128,1,256]{2,1,0:T(1,128)}), f32[128,1,256]{2,1,0:T(1,128)S(1)}, u32[]{:S(2)}, u32[]{:S(2)}) async-start(f32[128,1,256]{2,1,0:T(1,128)} %all_to_all.18), calls=%async_computation | async-start | bytes 262144 | tf_op jit(solution)/shard_map/all_to_all | solution.py:54
  29.1 0.7 copy-start.3
  44.0 3.6 %collective-permute-start = (f32[128,256]{1,0:T(8,128)S(1)}, f32[128,256]{1,0:T(8,128)S(1)}, u32[]{:S(2)}, u32[]{:S(2)}) collective-permute-start(f32[128,256]{1,0:T(8,128)S(1)} %bitcast.43), channel_id=1, source_target_pairs={{0,4},{4,0},{8,12},{12,8},{16,20},{20,16},{24,28},{28,24},{32,36},... | collective-permute-start | bytes 393224 | tf_op jit(solution)/shard_map/ppermute | solution.py:55
  88.0 0.7 copy-start.2

commit v8 on v6

--- a/solution.py
+++ b/solution.py
@@ -39,6 +39,8 @@
     chan = own // dup
     half = own % dup
     signal_f = signal.astype(jnp.float32)
+    gains = jnp.broadcast_to(norm_gain[:, None], signal.shape)
+    gains, signal_f = lax.optimization_barrier((gains, signal_f))
 
     both = jnp.stack([signal_f, long_filter], 1)
     mine = lax.all_to_all(both.reshape(seq_parts, length), "seq", 0, 0, tiled=True)
@@ -93,7 +95,7 @@
     spread = jnp.broadcast_to(partial[None], (groups,) + partial.shape)
     energy = jnp.sum(lax.all_to_all(spread, "ch", 0, 0, tiled=True), 0)
     all_channels = width * groups
-    return short_local * norm_gain[:, None] * lax.rsqrt(energy / all_channels + 1e-06)[None, :]
+    return short_local * gains * lax.rsqrt(energy / all_channels + 1e-06)[None, :]
 
 
 def solution(mesh):

time: 88.5 us -> 87.8 us (level)
  no operation moved by 1% of the time
where the time goes in v8:
time: 87.8 us; the launch traced here: 87.4 us
  blocking collectives  32.3 us (37%)
  starting transfers between devices  25.6 us (29%)
  waiting for transfers between devices  10.9 us (12%)
  other arithmetic  8.91 us (10%)
  matrix products  5.79 us (7%)
  local copies, waits for them, and re-layouts  3.54 us (4%)
    all_to_all x1, blocking collectives, local(): got = lax.all_to_all(back, 'seq', 0, 0, tiled=True)  24.5 us
    all_to_all x1, starting transfers between devices, local(): lax.all_to_all(both.reshape(seq_parts, length), 'seq', 0, 0, tiled=True)  23 us
    all_to_all x1, waiting for transfers between devices, local(): lax.all_to_all(both.reshape(seq_parts, length), 'seq', 0, 0, tiled=True)  10.5 us
    all_to_all x1, blocking collectives, local(): energy = jnp.sum(lax.all_to_all(spread, 'ch', 0, 0, tiled=True), 0)  7.81 us
    dot_general x19, matrix products, mat(): return jnp.dot(a, b, precision=highest, preferred_element_type=jnp.float32)  5.79 us
    add x1, other arithmetic, local(): band = band + jnp.where(lag == offset, taps[offset], 0.0)  4.51 us
    ppermute x1, starting transfers between devices, local(): other = lax.ppermute(mine, 'seq', [(i, i ^ 1) for i in range(seq_parts)])  2.62 us
    sin x2, other arithmetic, phases(): return (jnp.cos(angles), direction * jnp.sin(angles))  2.07 us
  transfers between devices with their start and end apart: 2, of which 2 were waited for; matrix products, arithmetic and copies ran while one was open for 10% of the time, Pallas kernels for 0%

profile of v8, /device:TPU:1, one launch (start us, length us, event | category | flops | bytes accessed | tf_op | source)
XLA Modules:
  0.0 87.4 jit_solution(6348840985913815091)
XLA Ops:
  0.0 0.8 convert_element_type.15
  1.0 0.8 all_to_all.18
  1.9 23.0 %all-to-all-start = ((f32[128,1,256]{2,1,0:T(1,128)}), f32[128,1,256]{2,1,0:T(1,128)S(1)}, u32[]{:S(2)}, u32[]{:S(2)}) async-start(f32[128,1,256]{2,1,0:T(1,128)} %all_to_all.18), calls=%async_computation | async-start | bytes 262144 | tf_op jit(solution)/shard_map/all_to_all | solution.py:46
  24.9 1.0 %fusion.36 = (f32[256,256]{1,0:T(8,128)S(1)}, f32[256,256]{1,0:T(8,128)S(1)}) fusion(), kind=kLoop, calls=%fused_computation.65 | loop fusion | flops 917504 | bytes 524288 | tf_op jit(solution)/shard_map/sin | solution.py:14
  25.9 1.0 %fusion.38 = (f32[256,256]{1,0:T(8,128)S(1)}, f32[256,256]{1,0:T(8,128)S(1)}) fusion(), kind=kLoop, calls=%fused_computation.67 | loop fusion | flops 917504 | bytes 524288 | tf_op jit(solution)/shard_map/sin | solution.py:14
  27.0 0.6 copy-done.3
  27.7 0.6 dynamic_slice.8
  28.4 0.6 fusion.49
  29.0 4.5 %select_add_fusion = f32[512,128]{1,0:T(8,128)S(1)} fusion(f32[]{:T(128)} %bitcast.9, f32[]{:T(128)} %bitcast.8, f32[]{:T(128)} %bitcast.7, f32[]{:T(128)} %bitcast.6, f32[]{:T(128)} %bitcast.5, f32[]{:T(128)} %bitcast.4, f32[]{:T(128)} %bitcast.3, s32[512]{0:T(512)S(1)} %compare_select_fusion, s32[128]{0:T(128)S(1)} %iota_add_fusion), kind=kLoop, calls=%fused_computation.29 | loop fusion | flops 1376256 | bytes 264732 | tf_op jit(solution)/shard_map/add | solution.py:87
  33.5 10.5 %all-to-all-done = f32[128,1,256]{2,1,0:T(1,128)S(1)} async-done(((f32[128,1,256]{2,1,0:T(1,128)}), f32[128,1,256]{2,1,0:T(1,128)S(1)}, u32[]{:S(2)}, u32[]{:S(2)}) %all-to-all-start) | async-done | bytes 131104 | tf_op jit(solution)/shard_map/all_to_all | solution.py:46
  44.0 2.6 %collective-permute-start = (f32[128,256]{1,0:T(8,128)S(1)}, f32[128,256]{1,0:T(8,128)S(1)}, u32[]{:S(2)}, u32[]{:S(2)}) collective-permute-start(f32[128,256]{1,0:T(8,128)S(1)} %bitcast.47), channel_id=1, source_target_pairs={{0,4},{4,0},{8,12},{12,8},{16,20},{20,16},{24,28},{28,24},{32,36},... | collective-permute-start | bytes 393224 | tf_op jit(solution)/shard_map/ppermute | solution.py:47
  47.2 0.4 collective-permute-done
  47.9 0.3 multiply_add_fusion.1
  48.2 0.3 fusion.22
  48.5 0.3 fusion.51
  48.7 0.3 fusion.50
  49.0 0.3 fusion.24
  49.3 0.3 convolution_add_fusion.1
  49.6 0.3 convolution_subtract_fusion.1
  49.9 0.3 convolution_subtract_fusion.2
  50.2 0.3 multiply_add_fusion
  50.5 0.3 fusion.52
  50.8 0.3 fusion.53
  51.1 0.3 convolution_subtract_fusion
  51.3 0.3 convolution_add_fusion
  51.9 0.9 %multiply_add_fusion.3 = f32[128,256]{1,0:T(8,128)S(1)} fusion(f32[128,256]{1,0:T(8,128)S(1)} %collective-permute-done, f32[128,256]{1,0:T(8,128)S(1)} %fusion.11, f32[256,256]{1,0:T(8,128)S(1)} %convolution_add_fusion, f32[256,256]{1,0:T(8,128)S(1)} %get-tuple-element.13, f32[256,256]{1,0:T(8,128)S(1)} %convolution_subtract_fusion, ...), kind=kOutput, calls=%fused_computation.61 | convolution fusion | flops 50692096 | bytes 1703941 | tf_op jit(solution)/shard_map/dot_general | solution.py:18
  52.8 0.3 fusion.5
  53.0 24.5 %all_to_all.27 = f32[128,1,128]{2,1,0:T(1,128)S(1)} all-to-all(f32[128,1,128]{2,1,0:T(1,128)S(1)} %bitcast.45), channel_id=1, replica_groups=mesh['seq'=128,'ch'=4] {'seq'}, dimensions={0} | all-to-all | bytes 131072 | tf_op jit(solution)/shard_map/all_to_all | solution.py:90
  77.5 0.5 broadcast.67
  78.0 0.8 reduce.4
  78.9 7.8 %all_to_all.28 = f32[4,1,256]{2,1,0:T(1,128)S(1)} all-to-all(f32[4,1,256]{2,1,0:T(1,128)S(1)} %broadcast_in_dim.61), channel_id=1, replica_groups=mesh['seq'=128,'ch'=4] {'ch'}, dimensions={0} | all-to-all | bytes 8192 | tf_op jit(solution)/shard_map/all_to_all | solution.py:96
  86.8 0.6 multiply_multiply_fusion
  (23 shorter events, 1.4 us)
Async XLA Ops:
  0.0 28.3 %copy-start = (f32[7,64]{1,0:T(8,128)S(1)}, f32[7,64]{1,0:T(8,128)}, u32[]{:S(2)}) copy-start(f32[7,64]{1,0:T(8,128)} %param.8) | copy-start | bytes 5380
  0.0 0.8 copy-start.2
  0.0 0.9 %copy-start.1 = (f32[64,256]{1,0:T(8,128)S(1)}, f32[64,256]{1,0:T(8,128)}, u32[]{:S(2)}) copy-start(f32[64,256]{1,0:T(8,128)} %param.6) | copy-start | bytes 196612
  1.9 42.1 %all-to-all-start = ((f32[128,1,256]{2,1,0:T(1,128)}), f32[128,1,256]{2,1,0:T(1,128)S(1)}, u32[]{:S(2)}, u32[]{:S(2)}) async-start(f32[128,1,256]{2,1,0:T(1,128)} %all_to_all.18), calls=%async_computation | async-start | bytes 262144 | tf_op jit(solution)/shard_map/all_to_all | solution.py:46
  27.0 0.7 copy-start.3
  44.0 3.6 %collective-permute-start = (f32[128,256]{1,0:T(8,128)S(1)}, f32[128,256]{1,0:T(8,128)S(1)}, u32[]{:S(2)}, u32[]{:S(2)}) collective-permute-start(f32[128,256]{1,0:T(8,128)S(1)} %bitcast.47), channel_id=1, source_target_pairs={{0,4},{4,0},{8,12},{12,8},{16,20},{20,16},{24,28},{28,24},{32,36},... | collective-permute-start | bytes 393224 | tf_op jit(solution)/shard_map/ppermute | solution.py:47

commit v9 on v8

--- a/solution.py
+++ b/solution.py
@@ -91,7 +91,8 @@
     short_local = got.reshape(width, length)
 
     groups = lax.axis_size("ch")
-    partial = jnp.sum(short_local * short_local, 0)
+    folded = got.reshape(width, dup, piece)
+    partial = jnp.sum(folded * folded, 0).reshape(length)
     spread = jnp.broadcast_to(partial[None], (groups,) + partial.shape)
     energy = jnp.sum(lax.all_to_all(spread, "ch", 0, 0, tiled=True), 0)
     all_channels = width * groups

time: 87.8 us -> 88.7 us (1.010)
  blocking collectives: 32.3 us -> 24.6 us
  waiting for transfers between devices: 10.9 us -> 15.2 us
  starting transfers between devices: 25.6 us -> 29.2 us
    all_to_all x1 -> x0, blocking collectives: 7.81 us -> none  [local(): energy = jnp.sum(lax.all_to_all(spread, 'ch', 0, 0, tiled=True), 0)]
    all_to_all x0 -> x1, waiting for transfers between devices: none -> 4.4 us  [local(): energy = jnp.sum(lax.all_to_all(spread, 'ch', 0, 0, tiled=True), 0)]
    all_to_all x0 -> x1, starting transfers between devices: none -> 3.58 us  [local(): energy = jnp.sum(lax.all_to_all(spread, 'ch', 0, 0, tiled=True), 0)]
  transfers between devices with their start and end apart: 2 -> 3, of which waited for: 2 -> 3; matrix products, arithmetic and copies ran while one was open for 10% -> 10% of each run, Pallas kernels for 0% -> 0%
where the time goes in v9:
time: 88.7 us; the launch traced here: 88.4 us
  starting transfers between devices  29.2 us (33%)
  blocking collectives  24.6 us (28%)
  waiting for transfers between devices  15.2 us (17%)
  other arithmetic  9.09 us (10%)
  matrix products  5.81 us (7%)
  local copies, waits for them, and re-layouts  4.12 us (5%)
    all_to_all x1, blocking collectives, local(): got = lax.all_to_all(back, 'seq', 0, 0, tiled=True)  24.6 us
    all_to_all x1, starting transfers between devices, local(): lax.all_to_all(both.reshape(seq_parts, length), 'seq', 0, 0, tiled=True)  23 us
    all_to_all x1, waiting for transfers between devices, local(): lax.all_to_all(both.reshape(seq_parts, length), 'seq', 0, 0, tiled=True)  10.4 us
    dot_general x19, matrix products, mat(): return jnp.dot(a, b, precision=highest, preferred_element_type=jnp.float32)  5.81 us
    add x1, other arithmetic, local(): band = band + jnp.where(lag == offset, taps[offset], 0.0)  4.62 us
    all_to_all x1, waiting for transfers between devices, local(): energy = jnp.sum(lax.all_to_all(spread, 'ch', 0, 0, tiled=True), 0)  4.4 us
    all_to_all x1, starting transfers between devices, local(): energy = jnp.sum(lax.all_to_all(spread, 'ch', 0, 0, tiled=True), 0)  3.58 us
    ppermute x1, starting transfers between devices, local(): other = lax.ppermute(mine, 'seq', [(i, i ^ 1) for i in range(seq_parts)])  2.62 us
  transfers between devices with their start and end apart: 3, of which 3 were waited for; matrix products, arithmetic and copies ran while one was open for 10% of the time, Pallas kernels for 0%

profile of v9, /device:TPU:1, one launch (start us, length us, event | category | flops | bytes accessed | tf_op | source)
XLA Modules:
  0.0 88.4 jit_solution(17223956185530130549)
XLA Ops:
  0.0 0.8 convert_element_type.15
  1.0 0.8 all_to_all.18
  1.9 23.0 %all-to-all-start = ((f32[128,1,256]{2,1,0:T(1,128)}), f32[128,1,256]{2,1,0:T(1,128)S(1)}, u32[]{:S(2)}, u32[]{:S(2)}) async-start(f32[128,1,256]{2,1,0:T(1,128)} %all_to_all.18), calls=%async_computation | async-start | bytes 262144 | tf_op jit(solution)/shard_map/all_to_all | solution.py:46
  24.9 1.0 %fusion.36 = (f32[256,256]{1,0:T(8,128)S(1)}, f32[256,256]{1,0:T(8,128)S(1)}) fusion(), kind=kLoop, calls=%fused_computation.65 | loop fusion | flops 917504 | bytes 524288 | tf_op jit(solution)/shard_map/sin | solution.py:14
  25.9 1.0 %fusion.38 = (f32[256,256]{1,0:T(8,128)S(1)}, f32[256,256]{1,0:T(8,128)S(1)}) fusion(), kind=kLoop, calls=%fused_computation.67 | loop fusion | flops 917504 | bytes 524288 | tf_op jit(solution)/shard_map/sin | solution.py:14
  27.0 0.6 copy-done.3
  27.7 0.6 dynamic_slice.8
  28.4 0.6 fusion.50
  29.0 4.6 %select_add_fusion = f32[512,128]{1,0:T(8,128)S(1)} fusion(f32[]{:T(128)} %bitcast.9, f32[]{:T(128)} %bitcast.8, f32[]{:T(128)} %bitcast.7, f32[]{:T(128)} %bitcast.6, f32[]{:T(128)} %bitcast.5, f32[]{:T(128)} %bitcast.4, f32[]{:T(128)} %bitcast.3, s32[512]{0:T(512)S(1)} %compare_select_fusion, s32[128]{0:T(128)S(1)} %iota_add_fusion), kind=kLoop, calls=%fused_computation.29 | loop fusion | flops 1376256 | bytes 264732 | tf_op jit(solution)/shard_map/add | solution.py:87
  33.6 10.4 %all-to-all-done = f32[128,1,256]{2,1,0:T(1,128)S(1)} async-done(((f32[128,1,256]{2,1,0:T(1,128)}), f32[128,1,256]{2,1,0:T(1,128)S(1)}, u32[]{:S(2)}, u32[]{:S(2)}) %all-to-all-start) | async-done | bytes 131104 | tf_op jit(solution)/shard_map/all_to_all | solution.py:46
  44.0 2.6 %collective-permute-start = (f32[128,256]{1,0:T(8,128)S(1)}, f32[128,256]{1,0:T(8,128)S(1)}, u32[]{:S(2)}, u32[]{:S(2)}) collective-permute-start(f32[128,256]{1,0:T(8,128)S(1)} %bitcast.50), channel_id=1, source_target_pairs={{0,4},{4,0},{8,12},{12,8},{16,20},{20,16},{24,28},{28,24},{32,36},... | collective-permute-start | bytes 393224 | tf_op jit(solution)/shard_map/ppermute | solution.py:47
  47.2 0.4 collective-permute-done
  47.9 0.3 multiply_add_fusion.1
  48.2 0.3 fusion.22
  48.5 0.3 fusion.52
  48.7 0.3 fusion.51
  49.0 0.3 fusion.24
  49.3 0.3 convolution_add_fusion.1
  49.6 0.3 convolution_subtract_fusion.1
  49.9 0.3 convolution_subtract_fusion.2
  50.2 0.3 multiply_add_fusion
  50.5 0.3 fusion.53
  51.1 0.3 convolution_subtract_fusion
  51.3 0.3 convolution_add_fusion
  51.9 0.9 multiply_add_fusion.3
  53.0 24.6 %all_to_all.27 = f32[128,1,128]{2,1,0:T(1,128)S(1)} all-to-all(f32[128,1,128]{2,1,0:T(1,128)S(1)} %bitcast.48), channel_id=1, replica_groups=mesh['seq'=128,'ch'=4] {'seq'}, dimensions={0} | all-to-all | bytes 131072 | tf_op jit(solution)/shard_map/all_to_all | solution.py:90
  77.6 0.5 broadcast.67
  78.2 0.8 fusion.49
  79.1 0.6 broadcast_in_dim.63
  79.7 3.6 %all-to-all-start.2 = ((f32[4,1,256]{2,1,0:T(1,128)}), f32[4,1,256]{2,1,0:T(1,128)S(1)}, u32[]{:S(2)}, u32[]{:S(2)}) async-start(f32[4,1,256]{2,1,0:T(1,128)} %broadcast_in_dim.63), calls=%async_computation.2 | async-start | bytes 8192 | tf_op jit(solution)/shard_map/all_to_all | solution.py:97
  83.3 4.4 %all-to-all-done.2 = f32[4,1,256]{2,1,0:T(1,128)S(1)} async-done(((f32[4,1,256]{2,1,0:T(1,128)}), f32[4,1,256]{2,1,0:T(1,128)S(1)}, u32[]{:S(2)}, u32[]{:S(2)}) %all-to-all-start.2) | async-done | bytes 4128 | tf_op jit(solution)/shard_map/all_to_all | solution.py:97
  87.7 0.6 multiply_multiply_fusion
  (24 shorter events, 2.0 us)
Async XLA Ops:
  0.0 28.3 %copy-start = (f32[7,64]{1,0:T(8,128)S(1)}, f32[7,64]{1,0:T(8,128)}, u32[]{:S(2)}) copy-start(f32[7,64]{1,0:T(8,128)} %param.8) | copy-start | bytes 5380
  0.0 0.8 copy-start.2
  0.0 0.9 copy-start.1
  1.9 42.1 %all-to-all-start = ((f32[128,1,256]{2,1,0:T(1,128)}), f32[128,1,256]{2,1,0:T(1,128)S(1)}, u32[]{:S(2)}, u32[]{:S(2)}) async-start(f32[128,1,256]{2,1,0:T(1,128)} %all_to_all.18), calls=%async_computation | async-start | bytes 262144 | tf_op jit(solution)/shard_map/all_to_all | solution.py:46
  27.0 0.7 copy-start.3
  44.0 3.6 %collective-permute-start = (f32[128,256]{1,0:T(8,128)S(1)}, f32[128,256]{1,0:T(8,128)S(1)}, u32[]{:S(2)}, u32[]{:S(2)}) collective-permute-start(f32[128,256]{1,0:T(8,128)S(1)} %bitcast.50), channel_id=1, source_target_pairs={{0,4},{4,0},{8,12},{12,8},{16,20},{20,16},{24,28},{28,24},{32,36},... | collective-permute-start | bytes 393224 | tf_op jit(solution)/shard_map/ppermute | solution.py:47
  79.7 8.0 %all-to-all-start.2 = ((f32[4,1,256]{2,1,0:T(1,128)}), f32[4,1,256]{2,1,0:T(1,128)S(1)}, u32[]{:S(2)}, u32[]{:S(2)}) async-start(f32[4,1,256]{2,1,0:T(1,128)} %broadcast_in_dim.63), calls=%async_computation.2 | async-start | bytes 8192 | tf_op jit(solution)/shard_map/all_to_all | solution.py:97

commit v10 on v8

v10 whole, which is shorter than its diff:
```python
import math

import jax
import jax.numpy as jnp
from jax import lax
from jax.sharding import PartitionSpec as P

highest = lax.Precision.HIGH


def phases(left_ids, right_ids, modulus, direction):
    product = left_ids[:, None] * right_ids[None, :] % modulus
    angles = product.astype(jnp.float32) * (2.0 * math.pi / modulus)
    return (jnp.cos(angles), direction * jnp.sin(angles))


def mat(a, b):
    return jnp.dot(a, b, precision=highest, preferred_element_type=jnp.float32)


def cmat(ar, ai, br, bi):
    if ai is None:
        return (mat(ar, br), mat(ar, bi))
    if bi is None:
        return (mat(ar, br), mat(ai, br))
    return (mat(ar, br) - mat(ai, bi), mat(ar, bi) + mat(ai, br))


def cmul(ar, ai, br, bi):
    return (ar * br - ai * bi, ar * bi + ai * br)


def local(signal, long_filter, skip_weight, short_taps, norm_gain):
    chips = lax.axis_size("chip")
    width, length = signal.shape
    chan = lax.axis_index("chip")
    half = lax.axis_index("core")
    signal_f = signal.astype(jnp.float32)
    gains = jnp.broadcast_to(norm_gain[:, None], signal.shape)
    gains, signal_f = lax.optimization_barrier((gains, signal_f))

    both = jnp.stack([signal_f, long_filter], 1)
    mine = lax.all_to_all(both, "chip", 0, 0, tiled=True)
    other = lax.ppermute(mine, "core", [(0, 1), (1, 0)])

    seq_parts = 2 * chips
    rows = 2 * seq_parts
    cols = length
    modulus = rows * cols
    row_ids = jnp.arange(rows, dtype=jnp.int32)
    col_ids = jnp.arange(cols, dtype=jnp.int32)
    chip_ids = jnp.arange(chips, dtype=jnp.int32)
    square = phases(col_ids, col_ids, cols, 1.0)
    turn = phases(row_ids, col_ids, modulus, 1.0)
    rows_mine = phases(row_ids, 2 * chip_ids + half, rows, -1.0)
    rows_other = phases(row_ids, 2 * chip_ids + 1 - half, rows, -1.0)
    parity_ids = jnp.concatenate([2 * chip_ids, 2 * chip_ids + 1])
    rows_inv = phases(parity_ids, row_ids, rows, 1.0)
    square, turn, rows_mine, rows_other, rows_inv = lax.optimization_barrier(
        (square, turn, rows_mine, rows_other, rows_inv)
    )
    turn_fwd = (turn[0], -turn[1])
    cols_fwd = (square[0], -square[1])
    cols_inv = square

    def forward(own_rows, other_rows):
        yr = mat(rows_mine[0], own_rows) + mat(rows_other[0], other_rows)
        yi = mat(rows_mine[1], own_rows) + mat(rows_other[1], other_rows)
        yr, yi = cmul(yr, yi, turn_fwd[0], turn_fwd[1])
        return cmat(yr, yi, cols_fwd[0], cols_fwd[1])

    xr, xi = forward(mine[:, 0], other[:, 0])
    hr, hi = forward(mine[:, 1], other[:, 1])
    pr, pi = cmul(xr, xi, hr, hi)
    qr, qi = cmat(pr, pi, cols_inv[0], cols_inv[1])
    qr, qi = cmul(qr, qi, turn_fwd[0], -turn_fwd[1])
    conv = (mat(rows_inv[0], qr) - mat(rows_inv[1], qi)) * (1.0 / modulus)

    first = half == 0
    x_rows = jnp.where(
        first,
        jnp.concatenate([mine[:, 0], other[:, 0]], 0),
        jnp.concatenate([other[:, 0], mine[:, 0]], 0),
    )
    skip = lax.dynamic_index_in_dim(skip_weight, chan, keepdims=False)
    mixed = conv + skip * x_rows
    tap_count = short_taps.shape[0]
    taps = lax.dynamic_index_in_dim(short_taps, chan, axis=1, keepdims=False)
    even, odd = mixed[:chips], mixed[chips:]
    own_rows = jnp.where(first, even, odd)
    odd_before = jnp.concatenate([jnp.zeros((1, length), mixed.dtype), odd[:-1]], 0)
    earlier = jnp.where(first, odd_before, even)
    joined = jnp.concatenate([own_rows, earlier], 1)
    source = jnp.arange(2 * length, dtype=jnp.int32)
    source = jnp.where(source < length, source, source - 2 * length)
    lag = col_ids[None, :] - source[:, None]
    band = jnp.zeros(lag.shape, mixed.dtype)
    for offset in range(tap_count):
        band = band + jnp.where(lag == offset, taps[offset], 0.0)
    band = lax.optimization_barrier(band)
    back = mat(joined, band)
    short_local = lax.all_to_all(back, "chip", 0, 0, tiled=True)

    groups = lax.axis_size("ch")
    partial = jnp.sum(short_local * short_local, 0)
    spread = jnp.broadcast_to(partial[None], (groups,) + partial.shape)
    energy = jnp.sum(lax.all_to_all(spread, "ch", 0, 0, tiled=True), 0)
    all_channels = width * groups
    return short_local * gains * lax.rsqrt(energy / all_channels + 1e-06)[None, :]


def solution(mesh):
    seq_parts, groups = mesh.devices.shape
    split = jax.sharding.Mesh(mesh.devices.reshape(seq_parts // 2, 2, groups), ("chip", "core", "ch"))
    seq = ("chip", "core")
    return jax.shard_map(
        local,
        mesh=split,
        in_specs=(P("ch", seq), P("ch", seq), P("ch"), P(None, "ch"), P("ch")),
        out_specs=P("ch", seq),
        check_vma=False,
    )
```

time: 87.8 us -> 87.5 us (level)
  waiting for transfers between devices: 10.9 us -> 6.83 us
  other arithmetic: 8.91 us -> 10.9 us
  matrix products: 5.79 us -> 6.72 us
    all_to_all x1, waiting for transfers between devices: 10.5 us -> 6.82 us  [local(): mine = lax.all_to_all(both, 'chip', 0, 0, tiled=True)]
    ppermute x1, starting transfers between devices: 2.62 us -> 4.1 us  [local(): other = lax.ppermute(mine, 'core', [(0, 1), (1, 0)])]
    all_to_all x1, starting transfers between devices: 23 us -> 21.7 us  [local(): mine = lax.all_to_all(both, 'chip', 0, 0, tiled=True)]
    all_to_all x2, local copies, waits for them, and re-layouts: 1.35 us -> 0.08 us  [the longest x1 0.07 us: local(): short_local = lax.all_to_all(back, 'chip', 0, 0, tiled=True)]
    all_to_all x1, blocking collectives: 24.5 us -> 25.7 us  [local(): short_local = lax.all_to_all(back, 'chip', 0, 0, tiled=True)]
    mul x0 -> x3, other arithmetic: none -> 1.07 us  [the longest x2 1.07 us: phases(): return (jnp.cos(angles), direction * jnp.sin(angles))]
    dot_general x19 -> x23, matrix products: 5.79 us -> 6.72 us  [mat(): return jnp.dot(a, b, precision=highest, preferred_element_type=jnp.float32)]
    sin x2 -> x3, other arithmetic: 2.07 us -> 2.66 us  [phases(): return (jnp.cos(angles), direction * jnp.sin(angles))]
  transfers between devices with their start and end apart: 2 -> 2, of which waited for: 2 -> 1; matrix products, arithmetic and copies ran while one was open for 10% -> 13% of each run, Pallas kernels for 0% -> 0%
where the time goes in v10:
time: 87.5 us; the launch traced here: 86.6 us
  blocking collectives  32.9 us (38%)
  starting transfers between devices  25.8 us (29%)
  other arithmetic  10.9 us (12%)
  waiting for transfers between devices  6.83 us (8%)
  matrix products  6.72 us (8%)
  local copies, waits for them, and re-layouts  3.05 us (3%)
    all_to_all x1, blocking collectives, local(): short_local = lax.all_to_all(back, 'chip', 0, 0, tiled=True)  25.7 us
    all_to_all x1, starting transfers between devices, local(): mine = lax.all_to_all(both, 'chip', 0, 0, tiled=True)  21.7 us
    all_to_all x1, blocking collectives, local(): energy = jnp.sum(lax.all_to_all(spread, 'ch', 0, 0, tiled=True), 0)  7.14 us
    all_to_all x1, waiting for transfers between devices, local(): mine = lax.all_to_all(both, 'chip', 0, 0, tiled=True)  6.82 us
    dot_general x23, matrix products, mat(): return jnp.dot(a, b, precision=highest, preferred_element_type=jnp.float32)  6.72 us
    add x1, other arithmetic, local(): band = band + jnp.where(lag == offset, taps[offset], 0.0)  4.82 us
    ppermute x1, starting transfers between devices, local(): other = lax.ppermute(mine, 'core', [(0, 1), (1, 0)])  4.1 us
    sin x3, other arithmetic, phases(): return (jnp.cos(angles), direction * jnp.sin(angles))  2.66 us
  transfers between devices with their start and end apart: 2, of which 1 were waited for; matrix products, arithmetic and copies ran while one was open for 13% of the time, Pallas kernels for 0%

profile of v10, /device:TPU:1, one launch (start us, length us, event | category | flops | bytes accessed | tf_op | source)
XLA Modules:
  0.0 86.6 jit_solution(12557436051387053028)
XLA Ops:
  0.0 0.8 convert_element_type.27
  0.9 0.8 copy-done.1
  1.8 0.8 pad_maximum_fusion
  2.5 21.7 %all-to-all-start = ((f32[64,2,256]{2,1,0:T(2,128)}), f32[64,2,256]{2,1,0:T(2,128)S(1)}, u32[]{:S(2)}, u32[]{:S(2)}) async-start(f32[64,2,256]{2,1,0:T(2,128)} %pad_maximum_fusion), calls=%async_computation | async-start | bytes 262144 | tf_op jit(solution)/shard_map/all_to_all | solution.py:43
  24.3 1.0 %fusion.52 = (f32[256,256]{1,0:T(8,128)S(1)}, f32[256,256]{1,0:T(8,128)S(1)}) fusion(), kind=kLoop, calls=%fused_computation.91 | loop fusion | flops 917504 | bytes 524288 | tf_op jit(solution)/shard_map/sin | solution.py:14
  25.3 1.0 %fusion.54 = (f32[256,256]{1,0:T(8,128)S(1)}, f32[256,256]{1,0:T(8,128)S(1)}) fusion(), kind=kLoop, calls=%fused_computation.93 | loop fusion | flops 917504 | bytes 524288 | tf_op jit(solution)/shard_map/sin | solution.py:14
  26.4 0.5 sine_multiply_fusion
  26.9 0.5 sine_multiply_fusion.1
  27.5 0.6 fusion.65
  28.2 0.6 copy-done.3
  28.8 0.6 dynamic_slice.8
  29.5 0.6 fusion.74
  30.1 4.8 %select_add_fusion = f32[512,256]{1,0:T(8,128)S(1)} fusion(f32[]{:T(128)} %bitcast.10, f32[]{:T(128)} %bitcast.9, f32[]{:T(128)} %bitcast.8, f32[]{:T(128)} %bitcast.7, f32[]{:T(128)} %bitcast.6, f32[]{:T(128)} %bitcast.5, f32[]{:T(128)} %bitcast.4, s32[512]{0:T(512)S(1)} %compare_select_fusion), kind=kLoop, calls=%fused_computation.14 | loop fusion | flops 2752512 | bytes 526364 | tf_op jit(solution)/shard_map/add | solution.py:99
  34.9 6.8 %all-to-all-done = f32[64,2,256]{2,1,0:T(2,128)S(1)} async-done(((f32[64,2,256]{2,1,0:T(2,128)}), f32[64,2,256]{2,1,0:T(2,128)S(1)}, u32[]{:S(2)}, u32[]{:S(2)}) %all-to-all-start) | async-done | bytes 131104 | tf_op jit(solution)/shard_map/all_to_all | solution.py:43
  41.8 4.1 %collective-permute-start = (f32[64,2,256]{2,0,1:T(8,128)S(1)}, f32[64,2,256]{2,0,1:T(8,128)S(1)}, u32[]{:S(2)}, u32[]{:S(2)}) collective-permute-start(f32[64,2,256]{2,0,1:T(8,128)S(1)} %copy.12), channel_id=1, source_target_pairs={{0,4},{4,0},{1,5},{5,1},{2,6},{6,2},{3,7},{7,3},{8,12},{12,8},{9,1... | collective-permute-start | bytes 393224 | tf_op jit(solution)/shard_map/ppermute | solution.py:44
  47.7 0.3 multiply_add_fusion.1
  48.0 0.3 fusion.29
  48.3 0.3 fusion.27
  48.6 0.3 fusion.75
  48.9 0.3 fusion.76
  49.2 0.3 convolution_add_fusion.1
  49.5 0.3 convolution_subtract_fusion.1
  49.8 0.3 convolution_subtract_fusion.2
  50.1 0.3 multiply_add_fusion
  50.4 0.3 fusion.77
  50.9 0.3 convolution_subtract_fusion
  51.2 0.3 convolution_add_fusion
  51.8 0.8 fusion.1
  52.6 0.3 convolution_bitcast_fusion
  53.0 25.7 %all_to_all.23 = f32[64,1,256]{2,1,0:T(1,128)S(1)} all-to-all(f32[64,1,256]{2,1,0:T(1,128)S(1)} %copy.14), channel_id=1, replica_groups=mesh['chip'=64,'core'=2,'ch'=4] {'chip'}, dimensions={0} | all-to-all | bytes 131072 | tf_op jit(solution)/shard_map/all_to_all | solution.py:102
  78.7 7.1 %all_to_all.24 = f32[4,1,256]{2,1,0:T(1,128)S(1)} all-to-all(f32[4,1,256]{2,1,0:T(1,128)S(1)} %broadcast_in_dim.67), channel_id=1, replica_groups=mesh['chip'=64,'core'=2,'ch'=4] {'ch'}, dimensions={0} | all-to-all | bytes 8192 | tf_op jit(solution)/shard_map/all_to_all | solution.py:107
  85.9 0.6 fusion.59
  (35 shorter events, 2.8 us)
Async XLA Ops:
  0.0 29.4 %copy-start = (f32[7,64]{1,0:T(8,128)S(1)}, f32[7,64]{1,0:T(8,128)}, u32[]{:S(2)}) copy-start(f32[7,64]{1,0:T(8,128)} %param.8) | copy-start | bytes 5380
  0.0 0.8 copy-start.2
  0.9 0.8 copy-start.1
  2.5 39.2 %all-to-all-start = ((f32[64,2,256]{2,1,0:T(2,128)}), f32[64,2,256]{2,1,0:T(2,128)S(1)}, u32[]{:S(2)}, u32[]{:S(2)}) async-start(f32[64,2,256]{2,1,0:T(2,128)} %pad_maximum_fusion), calls=%async_computation | async-start | bytes 262144 | tf_op jit(solution)/shard_map/all_to_all | solution.py:43
  28.2 0.7 copy-start.3
  41.8 5.2 %collective-permute-start = (f32[64,2,256]{2,0,1:T(8,128)S(1)}, f32[64,2,256]{2,0,1:T(8,128)S(1)}, u32[]{:S(2)}, u32[]{:S(2)}) collective-permute-start(f32[64,2,256]{2,0,1:T(8,128)S(1)} %copy.12), channel_id=1, source_target_pairs={{0,4},{4,0},{1,5},{5,1},{2,6},{6,2},{3,7},{7,3},{8,12},{12,8},{9,1... | collective-permute-start | bytes 393224 | tf_op jit(solution)/shard_map/ppermute | solution.py:44

commit v11 on v10

--- a/solution.py
+++ b/solution.py
@@ -54,10 +54,15 @@
     turn = phases(row_ids, col_ids, modulus, 1.0)
     rows_mine = phases(row_ids, 2 * chip_ids + half, rows, -1.0)
     rows_other = phases(row_ids, 2 * chip_ids + 1 - half, rows, -1.0)
-    parity_ids = jnp.concatenate([2 * chip_ids, 2 * chip_ids + 1])
-    rows_inv = phases(parity_ids, row_ids, rows, 1.0)
-    square, turn, rows_mine, rows_other, rows_inv = lax.optimization_barrier(
-        (square, turn, rows_mine, rows_other, rows_inv)
+    rows_back = phases(2 * chip_ids + half, row_ids, rows, 1.0)
+    tap_count = short_taps.shape[0]
+    tap_ids = jnp.arange(tap_count, dtype=jnp.int32)
+    taps = lax.dynamic_index_in_dim(short_taps, chan, axis=1, keepdims=False)
+    tap_rows = phases(row_ids, tap_ids, modulus, -1.0)
+    tap_cols = phases(tap_ids, col_ids, cols, -1.0)
+    tap_spec = cmat(taps[None, :] * tap_rows[0], taps[None, :] * tap_rows[1], tap_cols[0], tap_cols[1])
+    square, turn, rows_mine, rows_other, rows_back, tap_spec = lax.optimization_barrier(
+        (square, turn, rows_mine, rows_other, rows_back, tap_spec)
     )
     turn_fwd = (turn[0], -turn[1])
     cols_fwd = (square[0], -square[1])
@@ -69,36 +74,25 @@
         yr, yi = cmul(yr, yi, turn_fwd[0], turn_fwd[1])
         return cmat(yr, yi, cols_fwd[0], cols_fwd[1])
 
+    skip = lax.dynamic_index_in_dim(skip_weight, chan, keepdims=False)
     xr, xi = forward(mine[:, 0], other[:, 0])
     hr, hi = forward(mine[:, 1], other[:, 1])
-    pr, pi = cmul(xr, xi, hr, hi)
+    pr, pi = cmul(xr, xi, hr + skip, hi)
+    pr, pi = cmul(pr, pi, tap_spec[0], tap_spec[1])
     qr, qi = cmat(pr, pi, cols_inv[0], cols_inv[1])
     qr, qi = cmul(qr, qi, turn_fwd[0], -turn_fwd[1])
-    conv = (mat(rows_inv[0], qr) - mat(rows_inv[1], qi)) * (1.0 / modulus)
+    back = (mat(rows_back[0], qr) - mat(rows_back[1], qi)) * (1.0 / modulus)
 
-    first = half == 0
-    x_rows = jnp.where(
-        first,
-        jnp.concatenate([mine[:, 0], other[:, 0]], 0),
-        jnp.concatenate([other[:, 0], mine[:, 0]], 0),
-    )
-    skip = lax.dynamic_index_in_dim(skip_weight, chan, keepdims=False)
-    mixed = conv + skip * x_rows
-    tap_count = short_taps.shape[0]
-    taps = lax.dynamic_index_in_dim(short_taps, chan, axis=1, keepdims=False)
-    even, odd = mixed[:chips], mixed[chips:]
-    own_rows = jnp.where(first, even, odd)
-    odd_before = jnp.concatenate([jnp.zeros((1, length), mixed.dtype), odd[:-1]], 0)
-    earlier = jnp.where(first, odd_before, even)
-    joined = jnp.concatenate([own_rows, earlier], 1)
-    source = jnp.arange(2 * length, dtype=jnp.int32)
-    source = jnp.where(source < length, source, source - 2 * length)
-    lag = col_ids[None, :] - source[:, None]
-    band = jnp.zeros(lag.shape, mixed.dtype)
-    for offset in range(tap_count):
-        band = band + jnp.where(lag == offset, taps[offset], 0.0)
-    band = lax.optimization_barrier(band)
-    back = mat(joined, band)
+    last = jnp.where(half == 1, mine[chips - 1], other[chips - 1])
+    rim = tap_count - 2
+    x_end = last[0, length - rim :][::-1]
+    h_end = last[1, length - rim :][::-1]
+    wrapped = [sum(x_end[i] * h_end[q - i] for i in range(q + 1)) for q in range(rim)]
+    wrap = [
+        sum(taps[t + r] * wrapped[r - 2] for r in range(2, tap_count - t)) for t in range(rim)
+    ]
+    fix = jnp.stack(wrap) * (half == 0).astype(back.dtype)
+    back = back.at[0, :rim].add(-fix)
     short_local = lax.all_to_all(back, "chip", 0, 0, tiled=True)
 
     groups = lax.axis_size("ch")

time: 87.5 us -> 116 us (1.33)
  between operations: 0.35 us -> 28.4 us
  other arithmetic: 10.9 us -> 5.82 us
  matrix products: 6.72 us -> 9.46 us
  waiting for transfers between devices: 6.83 us -> 8.77 us
  local copies, waits for them, and re-layouts: 3.05 us -> 4.78 us
  blocking collectives: 32.9 us -> 31.4 us
    add x1 -> x0, other arithmetic: 4.82 us -> none  [local(): band = band + jnp.where(lag == offset, taps[offset], 0.0)]
    dot_general x23 -> x26, matrix products: 6.72 us -> 9.46 us  [mat(): return jnp.dot(a, b, precision=highest, preferred_element_type=jnp.float32)]
    all_to_all x1, waiting for transfers between devices: 6.82 us -> 8.24 us  [local(): mine = lax.all_to_all(both, 'chip', 0, 0, tiled=True)]
    all_to_all x1, blocking collectives: 25.7 us -> 24.3 us  [local(): short_local = lax.all_to_all(back, 'chip', 0, 0, tiled=True)]
  transfers between devices with their start and end apart: 2 -> 2, of which waited for: 1 -> 2; matrix products, arithmetic and copies ran while one was open for 13% -> 7% of each run, Pallas kernels for 0% -> 0%
where the time goes in v11:
time: 116 us; the launch traced here: 115 us
  blocking collectives  31.4 us (27%)
  between operations  28.4 us (24%)
  starting transfers between devices  26 us (22%)
  matrix products  9.46 us (8%)
  waiting for transfers between devices  8.77 us (8%)
  other arithmetic  5.82 us (5%)
  local copies, waits for them, and re-layouts  4.78 us (4%)
    all_to_all x1, blocking collectives, local(): short_local = lax.all_to_all(back, 'chip', 0, 0, tiled=True)  24.3 us
    all_to_all x1, starting transfers between devices, local(): mine = lax.all_to_all(both, 'chip', 0, 0, tiled=True)  21.7 us
    dot_general x26, matrix products, mat(): return jnp.dot(a, b, precision=highest, preferred_element_type=jnp.float32)  9.46 us
    all_to_all x1, waiting for transfers between devices, local(): mine = lax.all_to_all(both, 'chip', 0, 0, tiled=True)  8.24 us
    all_to_all x1, blocking collectives, local(): energy = jnp.sum(lax.all_to_all(spread, 'ch', 0, 0, tiled=True), 0)  7.12 us
    ppermute x1, starting transfers between devices, local(): other = lax.ppermute(mine, 'core', [(0, 1), (1, 0)])  4.28 us
    sin x3, other arithmetic, phases(): return (jnp.cos(angles), direction * jnp.sin(angles))  2.41 us
  transfers between devices with their start and end apart: 2, of which 2 were waited for; matrix products, arithmetic and copies ran while one was open for 7% of the time, Pallas kernels for 0%

profile of v11, /device:TPU:1, one launch (start us, length us, event | category | flops | bytes accessed | tf_op | source)
XLA Modules:
  0.0 114.7 jit_solution(12534907576687634804)
XLA Ops:
  0.0 0.8 convert_element_type.46
  0.9 0.6 copy-done.2
  1.6 0.8 pad_maximum_fusion
  2.4 21.7 %all-to-all-start = ((f32[64,2,256]{2,1,0:T(2,128)}), f32[64,2,256]{2,1,0:T(2,128)S(1)}, u32[]{:S(2)}, u32[]{:S(2)}) async-start(f32[64,2,256]{2,1,0:T(2,128)} %pad_maximum_fusion), calls=%async_computation | async-start | bytes 262144 | tf_op jit(solution)/shard_map/all_to_all | solution.py:43
  24.1 0.3 fusion.88
  24.5 0.5 sine_multiply_fusion.2
  25.0 0.7 copy-done.1
  25.9 0.7 fusion.48
  26.7 0.7 fusion.49
  27.4 0.5 sine_multiply_fusion.1
  27.9 0.7 convolution_add_fusion.7
  28.7 1.0 fusion.43
  29.7 0.6 copy-done.3
  30.4 0.6 dynamic_slice.9
  31.0 1.0 fusion.41
  32.0 0.7 convolution_subtract_fusion.3
  32.7 0.6 fusion.139
  33.3 8.2 %all-to-all-done = f32[64,2,256]{2,1,0:T(2,128)S(1)} async-done(((f32[64,2,256]{2,1,0:T(2,128)}), f32[64,2,256]{2,1,0:T(2,128)S(1)}, u32[]{:S(2)}, u32[]{:S(2)}) %all-to-all-start) | async-done | bytes 131104 | tf_op jit(solution)/shard_map/all_to_all | solution.py:43
  42.4 4.3 %collective-permute-start = (f32[64,2,256]{2,1,0:T(2,128)S(1)}, f32[64,2,256]{2,1,0:T(2,128)S(1)}, u32[]{:S(2)}, u32[]{:S(2)}) collective-permute-start(f32[64,2,256]{2,1,0:T(2,128)S(1)} %all-to-all-done), channel_id=1, source_target_pairs={{0,4},{4,0},{1,5},{5,1},{2,6},{6,2},{3,7},{7,3},{8,12},{12,8},{9,1... | collective-permute-start | bytes 393224 | tf_op jit(solution)/shard_map/ppermute | solution.py:44
  47.0 0.5 collective-permute-done
  47.5 0.7 fusion.140
  73.3 0.3 multiply_add_fusion.2
  73.6 0.3 fusion.20
  73.9 0.3 fusion.142
  74.2 0.3 fusion.22
  74.8 0.3 convolution_add_fusion.1
  75.1 0.9 fusion
  76.0 0.3 convolution_subtract_fusion.2
  76.3 0.3 multiply_add_fusion
  82.6 24.3 %all_to_all.26 = f32[64,1,256]{2,1,0:T(1,128)S(1)} all-to-all(f32[64,1,256]{2,1,0:T(1,128)S(1)} %copy.13), channel_id=1, replica_groups=mesh['chip'=64,'core'=2,'ch'=4] {'chip'}, dimensions={0} | all-to-all | bytes 131072 | tf_op jit(solution)/shard_map/all_to_all | solution.py:96
  106.9 7.1 %all_to_all.27 = f32[4,1,256]{2,1,0:T(1,128)S(1)} all-to-all(f32[4,1,256]{2,1,0:T(1,128)S(1)} %broadcast_in_dim.5), channel_id=1, replica_groups=mesh['chip'=64,'core'=2,'ch'=4] {'ch'}, dimensions={0} | all-to-all | bytes 8192 | tf_op jit(solution)/shard_map/all_to_all | solution.py:101
  114.1 0.6 fusion.53
  (37 shorter events, 4.7 us)
Async XLA Ops:
  0.0 0.8 copy-start
  0.8 0.7 copy-start.2
  2.4 39.2 %all-to-all-start = ((f32[64,2,256]{2,1,0:T(2,128)}), f32[64,2,256]{2,1,0:T(2,128)S(1)}, u32[]{:S(2)}, u32[]{:S(2)}) async-start(f32[64,2,256]{2,1,0:T(2,128)} %pad_maximum_fusion), calls=%async_computation | async-start | bytes 262144 | tf_op jit(solution)/shard_map/all_to_all | solution.py:43
  25.0 0.7 copy-start.1
  29.7 0.7 copy-start.3
  42.4 5.1 %collective-permute-start = (f32[64,2,256]{2,1,0:T(2,128)S(1)}, f32[64,2,256]{2,1,0:T(2,128)S(1)}, u32[]{:S(2)}, u32[]{:S(2)}) collective-permute-start(f32[64,2,256]{2,1,0:T(2,128)S(1)} %all-to-all-done), channel_id=1, source_target_pairs={{0,4},{4,0},{1,5},{5,1},{2,6},{6,2},{3,7},{7,3},{8,12},{12,8},{9,1... | collective-permute-start | bytes 393224 | tf_op jit(solution)/shard_map/ppermute | solution.py:44

commit v12 on v11

--- a/solution.py
+++ b/solution.py
@@ -87,11 +87,18 @@
     rim = tap_count - 2
     x_end = last[0, length - rim :][::-1]
     h_end = last[1, length - rim :][::-1]
-    wrapped = [sum(x_end[i] * h_end[q - i] for i in range(q + 1)) for q in range(rim)]
-    wrap = [
-        sum(taps[t + r] * wrapped[r - 2] for r in range(2, tap_count - t)) for t in range(rim)
-    ]
-    fix = jnp.stack(wrap) * (half == 0).astype(back.dtype)
+    near = jnp.arange(rim, dtype=jnp.int32)
+    pair_sum = near[:, None, None] + near[None, :, None]
+    wrapped = jnp.sum(
+        jnp.where(pair_sum == near[None, None, :], x_end[:, None, None] * h_end[None, :, None], 0.0),
+        (0, 1),
+    )
+    reach = pair_sum[:, :, 0] + 2
+    weights = jnp.zeros((rim, rim), taps.dtype)
+    for offset in range(2, tap_count):
+        weights = weights + jnp.where(reach == offset, taps[offset], 0.0)
+    wrap = jnp.sum(weights * wrapped[None, :], 1)
+    fix = wrap * (half == 0).astype(back.dtype)
     back = back.at[0, :rim].add(-fix)
     short_local = lax.all_to_all(back, "chip", 0, 0, tiled=True)
 

time: 116 us -> 90.4 us (0.78)
  between operations: 28.4 us -> 0.36 us
  other arithmetic: 5.82 us -> 9.11 us
    reduce_sum x0 -> x2, other arithmetic: none -> 3.2 us  [the longest x1 3.11 us: local(): wrap = jnp.sum(weights * wrapped[None, :], 1)]
  transfers between devices with their start and end apart: 2 -> 2, of which waited for: 2 -> 2; matrix products, arithmetic and copies ran while one was open for 7% -> 9% of each run, Pallas kernels for 0% -> 0%
where the time goes in v12:
time: 90.4 us; the launch traced here: 89.4 us
  blocking collectives  31.4 us (35%)
  starting transfers between devices  26 us (29%)
  matrix products  9.46 us (10%)
  other arithmetic  9.11 us (10%)
  waiting for transfers between devices  8.77 us (10%)
  local copies, waits for them, and re-layouts  4.28 us (5%)
    all_to_all x1, blocking collectives, local(): short_local = lax.all_to_all(back, 'chip', 0, 0, tiled=True)  24.3 us
    all_to_all x1, starting transfers between devices, local(): mine = lax.all_to_all(both, 'chip', 0, 0, tiled=True)  21.7 us
    dot_general x26, matrix products, mat(): return jnp.dot(a, b, precision=highest, preferred_element_type=jnp.float32)  9.46 us
    all_to_all x1, waiting for transfers between devices, local(): mine = lax.all_to_all(both, 'chip', 0, 0, tiled=True)  8.24 us
    all_to_all x1, blocking collectives, local(): energy = jnp.sum(lax.all_to_all(spread, 'ch', 0, 0, tiled=True), 0)  7.15 us
    ppermute x1, starting transfers between devices, local(): other = lax.ppermute(mine, 'core', [(0, 1), (1, 0)])  4.28 us
    reduce_sum x1, other arithmetic, local(): wrap = jnp.sum(weights * wrapped[None, :], 1)  3.11 us
    sin x3, other arithmetic, phases(): return (jnp.cos(angles), direction * jnp.sin(angles))  2.41 us
  transfers between devices with their start and end apart: 2, of which 2 were waited for; matrix products, arithmetic and copies ran while one was open for 9% of the time, Pallas kernels for 0%

profile of v12, /device:TPU:1, one launch (start us, length us, event | category | flops | bytes accessed | tf_op | source)
XLA Modules:
  0.0 89.4 jit_solution(18181634569394648735)
XLA Ops:
  0.0 0.8 convert_element_type.46
  0.9 0.6 copy-done.2
  1.6 0.8 pad_maximum_fusion
  2.4 21.7 %all-to-all-start = ((f32[64,2,256]{2,1,0:T(2,128)}), f32[64,2,256]{2,1,0:T(2,128)S(1)}, u32[]{:S(2)}, u32[]{:S(2)}) async-start(f32[64,2,256]{2,1,0:T(2,128)} %pad_maximum_fusion), calls=%async_computation | async-start | bytes 262144 | tf_op jit(solution)/shard_map/all_to_all | solution.py:43
  24.2 0.3 fusion.88
  24.5 0.5 sine_multiply_fusion.2
  25.1 0.7 copy-done.1
  25.9 0.7 fusion.48
  26.7 0.7 fusion.49
  27.4 1.0 %fusion.43 = (f32[256,256]{1,0:T(8,128)S(1)}, f32[256,256]{1,0:T(8,128)S(1)}) fusion(), kind=kLoop, calls=%fused_computation.84 | loop fusion | flops 917504 | bytes 524288 | tf_op jit(solution)/shard_map/sin | solution.py:14
  28.4 0.5 sine_multiply_fusion.1
  29.0 0.7 convolution_add_fusion.7
  29.7 1.0 %fusion.41 = (f32[256,256]{1,0:T(8,128)S(1)}, f32[256,256]{1,0:T(8,128)S(1)}) fusion(), kind=kLoop, calls=%fused_computation.82 | loop fusion | flops 917504 | bytes 524288 | tf_op jit(solution)/shard_map/sin | solution.py:14
  30.8 0.6 copy-done.3
  31.4 0.6 dynamic_slice.9
  32.0 0.7 convolution_subtract_fusion.3
  32.8 0.6 fusion.139
  33.4 8.2 %all-to-all-done = f32[64,2,256]{2,1,0:T(2,128)S(1)} async-done(((f32[64,2,256]{2,1,0:T(2,128)}), f32[64,2,256]{2,1,0:T(2,128)S(1)}, u32[]{:S(2)}, u32[]{:S(2)}) %all-to-all-start) | async-done | bytes 131104 | tf_op jit(solution)/shard_map/all_to_all | solution.py:43
  42.5 4.3 %collective-permute-start = (f32[64,2,256]{2,1,0:T(2,128)S(1)}, f32[64,2,256]{2,1,0:T(2,128)S(1)}, u32[]{:S(2)}, u32[]{:S(2)}) collective-permute-start(f32[64,2,256]{2,1,0:T(2,128)S(1)} %all-to-all-done), channel_id=1, source_target_pairs={{0,4},{4,0},{1,5},{5,1},{2,6},{6,2},{3,7},{7,3},{8,12},{12,8},{9,1... | collective-permute-start | bytes 393224 | tf_op jit(solution)/shard_map/ppermute | solution.py:44
  47.0 0.5 collective-permute-done
  48.4 0.3 multiply_add_fusion.2
  48.7 0.3 fusion.20
  49.3 0.3 fusion.22
  49.9 0.3 convolution_add_fusion.1
  50.1 0.9 %fusion = f32[256,256]{1,0:T(8,128)S(1)} fusion(f32[256,256]{1,0:T(8,128)S(1)} %fusion.141, f32[256,256]{1,0:T(8,128)S(1)} %get-tuple-element.50, f32[256,256]{1,0:T(8,128)S(1)} %get-tuple-element.40, f32[]{:T(128)} %bitcast), kind=kOutput, calls=%fused_computation.5 | convolution fusion | flops 100859904 | bytes 1048580 | tf_op jit(solution)/shard_map/dot_general | solution.py:18
  51.1 0.3 convolution_subtract_fusion.2
  51.4 0.3 multiply_add_fusion
  52.6 0.3 convolution_add_fusion
  53.9 3.1 %multiply_reduce_fusion = f32[5]{0:T(128)S(1)} fusion(f32[5]{0:T(128)S(1)} %select_reduce_fusion, f32[]{:T(128)} %bitcast.6, f32[]{:T(128)} %bitcast.5, f32[]{:T(128)} %bitcast.4, f32[]{:T(128)} %bitcast.3, f32[]{:T(128)} %bitcast.2), kind=kLoop, calls=%fused_computation.144 | loop fusion | flops 445 | bytes 60 | tf_op jit(solution)/shard_map/reduce_sum | solution.py:100
  57.3 24.3 %all_to_all.26 = f32[64,1,256]{2,1,0:T(1,128)S(1)} all-to-all(f32[64,1,256]{2,1,0:T(1,128)S(1)} %copy.12), channel_id=1, replica_groups=mesh['chip'=64,'core'=2,'ch'=4] {'chip'}, dimensions={0} | all-to-all | bytes 131072 | tf_op jit(solution)/shard_map/all_to_all | solution.py:103
  81.6 7.2 %all_to_all.27 = f32[4,1,256]{2,1,0:T(1,128)S(1)} all-to-all(f32[4,1,256]{2,1,0:T(1,128)S(1)} %broadcast_in_dim.80), channel_id=1, replica_groups=mesh['chip'=64,'core'=2,'ch'=4] {'ch'}, dimensions={0} | all-to-all | bytes 8192 | tf_op jit(solution)/shard_map/all_to_all | solution.py:108
  88.8 0.6 fusion.53
  (42 shorter events, 5.1 us)
Async XLA Ops:
  0.0 0.8 copy-start
  0.8 0.7 copy-start.2
  2.4 39.2 %all-to-all-start = ((f32[64,2,256]{2,1,0:T(2,128)}), f32[64,2,256]{2,1,0:T(2,128)S(1)}, u32[]{:S(2)}, u32[]{:S(2)}) async-start(f32[64,2,256]{2,1,0:T(2,128)} %pad_maximum_fusion), calls=%async_computation | async-start | bytes 262144 | tf_op jit(solution)/shard_map/all_to_all | solution.py:43
  25.0 0.7 copy-start.1
  30.8 0.7 copy-start.3
  42.5 5.1 %collective-permute-start = (f32[64,2,256]{2,1,0:T(2,128)S(1)}, f32[64,2,256]{2,1,0:T(2,128)S(1)}, u32[]{:S(2)}, u32[]{:S(2)}) collective-permute-start(f32[64,2,256]{2,1,0:T(2,128)S(1)} %all-to-all-done), channel_id=1, source_target_pairs={{0,4},{4,0},{1,5},{5,1},{2,6},{6,2},{3,7},{7,3},{8,12},{12,8},{9,1... | collective-permute-start | bytes 393224 | tf_op jit(solution)/shard_map/ppermute | solution.py:44

commit v13 on v10

--- a/solution.py
+++ b/solution.py
@@ -24,6 +24,16 @@
     if bi is None:
         return (mat(ar, br), mat(ai, br))
     return (mat(ar, br) - mat(ai, bi), mat(ar, bi) + mat(ai, br))
+
+
+def gauss(ar, ai, table):
+    br, bsum, bdiff = table
+    common = mat(ar + ai, br)
+    return (common - mat(ai, bsum), common + mat(ar, bdiff))
+
+
+def with_sums(br, bi):
+    return (br, br + bi, bi - br)
 
 
 def cmul(ar, ai, br, bi):
@@ -56,23 +66,23 @@
     rows_other = phases(row_ids, 2 * chip_ids + 1 - half, rows, -1.0)
     parity_ids = jnp.concatenate([2 * chip_ids, 2 * chip_ids + 1])
     rows_inv = phases(parity_ids, row_ids, rows, 1.0)
-    square, turn, rows_mine, rows_other, rows_inv = lax.optimization_barrier(
-        (square, turn, rows_mine, rows_other, rows_inv)
+    cols_fwd = with_sums(square[0], -square[1])
+    cols_inv = with_sums(square[0], square[1])
+    square, turn, rows_mine, rows_other, rows_inv, cols_fwd, cols_inv = lax.optimization_barrier(
+        (square, turn, rows_mine, rows_other, rows_inv, cols_fwd, cols_inv)
     )
     turn_fwd = (turn[0], -turn[1])
-    cols_fwd = (square[0], -square[1])
-    cols_inv = square
 
     def forward(own_rows, other_rows):
         yr = mat(rows_mine[0], own_rows) + mat(rows_other[0], other_rows)
         yi = mat(rows_mine[1], own_rows) + mat(rows_other[1], other_rows)
         yr, yi = cmul(yr, yi, turn_fwd[0], turn_fwd[1])
-        return cmat(yr, yi, cols_fwd[0], cols_fwd[1])
+        return gauss(yr, yi, cols_fwd)
 
     xr, xi = forward(mine[:, 0], other[:, 0])
     hr, hi = forward(mine[:, 1], other[:, 1])
     pr, pi = cmul(xr, xi, hr, hi)
-    qr, qi = cmat(pr, pi, cols_inv[0], cols_inv[1])
+    qr, qi = gauss(pr, pi, cols_inv)
     qr, qi = cmul(qr, qi, turn_fwd[0], -turn_fwd[1])
     conv = (mat(rows_inv[0], qr) - mat(rows_inv[1], qi)) * (1.0 / modulus)
 

time: 87.5 us -> 88.9 us (1.016)
  waiting for transfers between devices: 6.83 us -> 4.7 us
  other arithmetic: 10.9 us -> 13 us
  blocking collectives: 32.9 us -> 34.9 us
    all_to_all x1, waiting for transfers between devices: 6.82 us -> 4.7 us  [local(): mine = lax.all_to_all(both, 'chip', 0, 0, tiled=True)]
    sub x0 -> x2, other arithmetic: none -> 2.12 us  [with_sums(): return (br, br + bi, bi - br)]
    all_to_all x1, blocking collectives: 25.7 us -> 27.7 us  [local(): short_local = lax.all_to_all(back, 'chip', 0, 0, tiled=True)]
    sin x3 -> x2, other arithmetic: 2.66 us -> 1.62 us  [phases(): return (jnp.cos(angles), direction * jnp.sin(angles))]
    cos x0 -> x1, other arithmetic: none -> 0.96 us  [phases(): return (jnp.cos(angles), direction * jnp.sin(angles))]
    dot_general x23 -> x20, matrix products: 6.72 us -> 5.9 us  [mat(): return jnp.dot(a, b, precision=highest, preferred_element_type=jnp.float32)]
  transfers between devices with their start and end apart: 2 -> 2, of which waited for: 1 -> 1; matrix products, arithmetic and copies ran while one was open for 13% -> 15% of each run, Pallas kernels for 0% -> 0%
where the time goes in v13:
time: 88.9 us; the launch traced here: 87.9 us
  blocking collectives  34.9 us (39%)
  starting transfers between devices  26 us (29%)
  other arithmetic  13 us (15%)
  matrix products  5.9 us (7%)
  waiting for transfers between devices  4.7 us (5%)
  local copies, waits for them, and re-layouts  3.07 us (3%)
    all_to_all x1, blocking collectives, local(): short_local = lax.all_to_all(back, 'chip', 0, 0, tiled=True)  27.7 us
    all_to_all x1, starting transfers between devices, local(): mine = lax.all_to_all(both, 'chip', 0, 0, tiled=True)  21.7 us
    all_to_all x1, blocking collectives, local(): energy = jnp.sum(lax.all_to_all(spread, 'ch', 0, 0, tiled=True), 0)  7.16 us
    dot_general x20, matrix products, mat(): return jnp.dot(a, b, precision=highest, preferred_element_type=jnp.float32)  5.9 us
    add x1, other arithmetic, local(): band = band + jnp.where(lag == offset, taps[offset], 0.0)  4.87 us
    all_to_all x1, waiting for transfers between devices, local(): mine = lax.all_to_all(both, 'chip', 0, 0, tiled=True)  4.7 us
    ppermute x1, starting transfers between devices, local(): other = lax.ppermute(mine, 'core', [(0, 1), (1, 0)])  4.28 us
    sub x2, other arithmetic, with_sums(): return (br, br + bi, bi - br)  2.12 us
  transfers between devices with their start and end apart: 2, of which 1 were waited for; matrix products, arithmetic and copies ran while one was open for 15% of the time, Pallas kernels for 0%

profile of v13, /device:TPU:1, one launch (start us, length us, event | category | flops | bytes accessed | tf_op | source)
XLA Modules:
  0.0 87.9 jit_solution(10865228350675976879)
XLA Ops:
  0.0 0.8 convert_element_type.39
  0.9 0.8 copy-done.1
  1.8 0.8 pad_maximum_fusion
  2.5 21.7 %all-to-all-start = ((f32[64,2,256]{2,1,0:T(2,128)}), f32[64,2,256]{2,1,0:T(2,128)S(1)}, u32[]{:S(2)}, u32[]{:S(2)}) async-start(f32[64,2,256]{2,1,0:T(2,128)} %pad_maximum_fusion), calls=%async_computation | async-start | bytes 262144 | tf_op jit(solution)/shard_map/all_to_all | solution.py:53
  24.3 1.1 %negate_subtract_fusion = (f32[256,256]{1,0:T(8,128)S(1)}, f32[256,256]{1,0:T(8,128)S(1)}) fusion(), kind=kLoop, calls=%fused_computation.59 | loop fusion | flops 1114112 | bytes 524288 | tf_op jit(solution)/shard_map/sub | solution.py:36
  25.4 1.0 %fusion.52 = (f32[256,256]{1,0:T(8,128)S(1)}, f32[256,256]{1,0:T(8,128)S(1)}) fusion(), kind=kLoop, calls=%fused_computation.93 | loop fusion | flops 917504 | bytes 524288 | tf_op jit(solution)/shard_map/sin | solution.py:14
  26.4 1.1 %fusion.56 = (f32[256,256]{1,0:T(8,128)S(1)}, f32[256,256]{1,0:T(8,128)S(1)}) fusion(), kind=kLoop, calls=%fused_computation.97 | loop fusion | flops 1048576 | bytes 524288 | tf_op jit(solution)/shard_map/sub | solution.py:36
  27.5 1.0 %fusion.55 = f32[256,256]{1,0:T(8,128)S(1)} fusion(), kind=kLoop, calls=%fused_computation.96 | loop fusion | flops 917504 | bytes 262144 | tf_op jit(solution)/shard_map/cos | solution.py:14
  28.4 0.5 sine_multiply_fusion
  29.0 0.5 sine_multiply_fusion.1
  29.6 0.6 fusion.67
  30.2 0.6 copy-done.3
  30.9 0.6 dynamic_slice.8
  31.5 0.6 fusion.76
  32.2 4.9 %select_add_fusion = f32[512,256]{1,0:T(8,128)S(1)} fusion(f32[]{:T(128)} %bitcast.10, f32[]{:T(128)} %bitcast.9, f32[]{:T(128)} %bitcast.8, f32[]{:T(128)} %bitcast.7, f32[]{:T(128)} %bitcast.6, f32[]{:T(128)} %bitcast.5, f32[]{:T(128)} %bitcast.4, s32[512]{0:T(512)S(1)} %compare_select_fusion), kind=kLoop, calls=%fused_computation.14 | loop fusion | flops 2752512 | bytes 526364 | tf_op jit(solution)/shard_map/add | solution.py:109
  37.0 4.7 %all-to-all-done = f32[64,2,256]{2,1,0:T(2,128)S(1)} async-done(((f32[64,2,256]{2,1,0:T(2,128)}), f32[64,2,256]{2,1,0:T(2,128)S(1)}, u32[]{:S(2)}, u32[]{:S(2)}) %all-to-all-start) | async-done | bytes 131104 | tf_op jit(solution)/shard_map/all_to_all | solution.py:53
  41.8 4.3 %collective-permute-start = (f32[64,2,256]{2,0,1:T(8,128)S(1)}, f32[64,2,256]{2,0,1:T(8,128)S(1)}, u32[]{:S(2)}, u32[]{:S(2)}) collective-permute-start(f32[64,2,256]{2,0,1:T(8,128)S(1)} %copy.12), channel_id=1, source_target_pairs={{0,4},{4,0},{1,5},{5,1},{2,6},{6,2},{3,7},{7,3},{8,12},{12,8},{9,1... | collective-permute-start | bytes 393224 | tf_op jit(solution)/shard_map/ppermute | solution.py:54
  47.9 0.3 multiply_add_fusion.1
  48.2 0.3 fusion.22
  48.5 0.3 convolution_add_fusion.1
  48.8 0.3 convolution_subtract_fusion.1
  49.1 0.3 fusion.24
  49.3 0.3 convolution_subtract_fusion.2
  49.6 0.3 multiply_add_fusion
  49.9 0.3 fusion.20
  50.2 0.3 convolution_subtract_fusion
  50.5 0.3 convolution_add_fusion
  51.0 0.9 fusion.1
  52.0 0.3 convolution_bitcast_fusion
  52.3 27.7 %all_to_all.23 = f32[64,1,256]{2,1,0:T(1,128)S(1)} all-to-all(f32[64,1,256]{2,1,0:T(1,128)S(1)} %copy.14), channel_id=1, replica_groups=mesh['chip'=64,'core'=2,'ch'=4] {'chip'}, dimensions={0} | all-to-all | bytes 131072 | tf_op jit(solution)/shard_map/all_to_all | solution.py:112
  80.1 7.2 %all_to_all.24 = f32[4,1,256]{2,1,0:T(1,128)S(1)} all-to-all(f32[4,1,256]{2,1,0:T(1,128)S(1)} %broadcast_in_dim.67), channel_id=1, replica_groups=mesh['chip'=64,'core'=2,'ch'=4] {'ch'}, dimensions={0} | all-to-all | bytes 8192 | tf_op jit(solution)/shard_map/all_to_all | solution.py:117
  87.3 0.6 fusion.61
  (34 shorter events, 2.6 us)
Async XLA Ops:
  0.0 31.5 %copy-start = (f32[7,64]{1,0:T(8,128)S(1)}, f32[7,64]{1,0:T(8,128)}, u32[]{:S(2)}) copy-start(f32[7,64]{1,0:T(8,128)} %param.8) | copy-start | bytes 5380
  0.0 0.8 copy-start.2
  0.9 0.8 copy-start.1
  2.5 39.2 %all-to-all-start = ((f32[64,2,256]{2,1,0:T(2,128)}), f32[64,2,256]{2,1,0:T(2,128)S(1)}, u32[]{:S(2)}, u32[]{:S(2)}) async-start(f32[64,2,256]{2,1,0:T(2,128)} %pad_maximum_fusion), calls=%async_computation | async-start | bytes 262144 | tf_op jit(solution)/shard_map/all_to_all | solution.py:53
  30.2 0.7 copy-start.3
  41.8 5.4 %collective-permute-start = (f32[64,2,256]{2,0,1:T(8,128)S(1)}, f32[64,2,256]{2,0,1:T(8,128)S(1)}, u32[]{:S(2)}, u32[]{:S(2)}) collective-permute-start(f32[64,2,256]{2,0,1:T(8,128)S(1)} %copy.12), channel_id=1, source_target_pairs={{0,4},{4,0},{1,5},{5,1},{2,6},{6,2},{3,7},{7,3},{8,12},{12,8},{9,1... | collective-permute-start | bytes 393224 | tf_op jit(solution)/shard_map/ppermute | solution.py:54

commit v14 on v8

--- a/solution.py
+++ b/solution.py
@@ -44,7 +44,11 @@
 
     both = jnp.stack([signal_f, long_filter], 1)
     mine = lax.all_to_all(both.reshape(seq_parts, length), "seq", 0, 0, tiled=True)
-    other = lax.ppermute(mine, "seq", [(i, i ^ 1) for i in range(seq_parts)])
+    partners = [(i, i ^ 1) for i in range(seq_parts)]
+    split = seq_parts // 2
+    other_top = lax.ppermute(mine[:split], "seq", partners)
+    other_low = lax.ppermute(mine[split:], "seq", partners)
+    other = jnp.concatenate([other_top, other_low], 0)
     x_rows = jnp.where(half == 0, mine, other)
 
     rows = 2 * seq_parts
@@ -67,7 +71,10 @@
         return cmat(yr, yi, cols_fwd[0], cols_fwd[1])
 
     xr, xi = forward(mine)
-    hr, hi = forward(other)
+    top_r, top_i = cmat(rows_fwd[0][:, :split], rows_fwd[1][:, :split], other_top, None)
+    low_r, low_i = cmat(rows_fwd[0][:, split:], rows_fwd[1][:, split:], other_low, None)
+    yr, yi = cmul(top_r + low_r, top_i + low_i, turn_fwd[0], turn_fwd[1])
+    hr, hi = cmat(yr, yi, cols_fwd[0], cols_fwd[1])
     pr, pi = cmul(xr, xi, hr, hi)
     qr, qi = cmat(pr, pi, cols_inv[0], cols_inv[1])
     qr, qi = cmul(qr, qi, turn_fwd[0], -turn_fwd[1])

time: 87.8 us -> 90.2 us (1.027)
  starting transfers between devices: 25.6 us -> 27.6 us
    ppermute x1 -> x2, starting transfers between devices: 2.62 us -> 4.54 us  [the longest x1 2.62 us: local(): other_low = lax.ppermute(mine[split:], 'seq', partners)]
    dot_general x19 -> x21, matrix products: 5.79 us -> 6.36 us  [mat(): return jnp.dot(a, b, precision=highest, preferred_element_type=jnp.float32)]
  transfers between devices with their start and end apart: 2 -> 3, of which waited for: 2 -> 2; matrix products, arithmetic and copies ran while one was open for 10% -> 10% of each run, Pallas kernels for 0% -> 0%
where the time goes in v14:
time: 90.2 us; the launch traced here: 89.8 us
  blocking collectives  32.6 us (36%)
  starting transfers between devices  27.6 us (31%)
  waiting for transfers between devices  10.4 us (12%)
  other arithmetic  9.1 us (10%)
  matrix products  6.36 us (7%)
  local copies, waits for them, and re-layouts  3.51 us (4%)
    all_to_all x1, blocking collectives, local(): got = lax.all_to_all(back, 'seq', 0, 0, tiled=True)  24.8 us
    all_to_all x1, starting transfers between devices, local(): lax.all_to_all(both.reshape(seq_parts, length), 'seq', 0, 0, tiled=True)  23 us
    all_to_all x1, waiting for transfers between devices, local(): lax.all_to_all(both.reshape(seq_parts, length), 'seq', 0, 0, tiled=True)  10.3 us
    all_to_all x1, blocking collectives, local(): energy = jnp.sum(lax.all_to_all(spread, 'ch', 0, 0, tiled=True), 0)  7.81 us
    dot_general x21, matrix products, mat(): return jnp.dot(a, b, precision=highest, preferred_element_type=jnp.float32)  6.36 us
    add x1, other arithmetic, local(): band = band + jnp.where(lag == offset, taps[offset], 0.0)  4.69 us
    ppermute x1, starting transfers between devices, local(): other_low = lax.ppermute(mine[split:], 'seq', partners)  2.62 us
    sin x2, other arithmetic, phases(): return (jnp.cos(angles), direction * jnp.sin(angles))  2.07 us
  transfers between devices with their start and end apart: 3, of which 2 were waited for; matrix products, arithmetic and copies ran while one was open for 10% of the time, Pallas kernels for 0%

profile of v14, /device:TPU:1, one launch (start us, length us, event | category | flops | bytes accessed | tf_op | source)
XLA Modules:
  0.0 89.8 jit_solution(5337864972145548134)
XLA Ops:
  0.0 0.8 convert_element_type.15
  1.0 0.8 all_to_all.18
  1.9 23.0 %all-to-all-start = ((f32[128,1,256]{2,1,0:T(1,128)}), f32[128,1,256]{2,1,0:T(1,128)S(1)}, u32[]{:S(2)}, u32[]{:S(2)}) async-start(f32[128,1,256]{2,1,0:T(1,128)} %all_to_all.18), calls=%async_computation | async-start | bytes 262144 | tf_op jit(solution)/shard_map/all_to_all | solution.py:46
  24.9 1.0 %fusion.49 = (f32[256,256]{1,0:T(8,128)S(1)}, f32[256,256]{1,0:T(8,128)S(1)}) fusion(), kind=kLoop, calls=%fused_computation.79 | loop fusion | flops 917504 | bytes 524288 | tf_op jit(solution)/shard_map/sin | solution.py:14
  25.9 1.0 %fusion.51 = (f32[256,256]{1,0:T(8,128)S(1)}, f32[256,256]{1,0:T(8,128)S(1)}) fusion(), kind=kLoop, calls=%fused_computation.81 | loop fusion | flops 917504 | bytes 524288 | tf_op jit(solution)/shard_map/sin | solution.py:14
  27.0 0.6 copy-done.3
  27.7 0.6 dynamic_slice.8
  28.3 0.6 fusion.59
  29.0 4.7 %select_add_fusion = f32[512,128]{1,0:T(8,128)S(1)} fusion(f32[]{:T(128)} %bitcast.11, f32[]{:T(128)} %bitcast.10, f32[]{:T(128)} %bitcast.9, f32[]{:T(128)} %bitcast.8, f32[]{:T(128)} %bitcast.7, f32[]{:T(128)} %bitcast.6, f32[]{:T(128)} %bitcast.5, s32[512]{0:T(512)S(1)} %compare_select_fusion, s32[128]{0:T(128)S(1)} %iota_add_fusion), kind=kLoop, calls=%fused_computation.31 | loop fusion | flops 1376256 | bytes 264732 | tf_op jit(solution)/shard_map/add | solution.py:94
  33.7 10.3 %all-to-all-done = f32[128,1,256]{2,1,0:T(1,128)S(1)} async-done(((f32[128,1,256]{2,1,0:T(1,128)}), f32[128,1,256]{2,1,0:T(1,128)S(1)}, u32[]{:S(2)}, u32[]{:S(2)}) %all-to-all-start) | async-done | bytes 131104 | tf_op jit(solution)/shard_map/all_to_all | solution.py:46
  44.0 2.6 %collective-permute-start.1 = (f32[64,256]{1,0:T(8,128)S(1)}, f32[64,256]{1,0:T(8,128)S(1)}, u32[]{:S(2)}, u32[]{:S(2)}) collective-permute-start(f32[64,256]{1,0:T(8,128)S(1)} %bitcast.54), channel_id=1, source_target_pairs={{0,4},{4,0},{8,12},{12,8},{16,20},{20,16},{24,28},{28,24},{32,36},... | collective-permute-start | bytes 196616 | tf_op jit(solution)/shard_map/ppermute | solution.py:50
  46.7 1.9 %collective-permute-start = (f32[64,256]{1,0:T(8,128)S(1)}, f32[64,256]{1,0:T(8,128)S(1)}, u32[]{:S(2)}, u32[]{:S(2)}) collective-permute-start(f32[64,256]{1,0:T(8,128)S(1)} %bitcast.55), channel_id=1, source_target_pairs={{0,4},{4,0},{8,12},{12,8},{16,20},{20,16},{24,28},{28,24},{32,36},... | collective-permute-start | bytes 196616 | tf_op jit(solution)/shard_map/ppermute | solution.py:49
  49.1 0.3 fusion.44
  49.4 0.3 fusion.30
  50.1 0.3 multiply_add_fusion.1
  50.4 0.3 fusion.24
  50.7 0.3 fusion.60
  50.9 0.3 fusion.22
  51.2 0.3 fusion.61
  51.5 0.3 convolution_add_fusion.1
  51.8 0.3 convolution_subtract_fusion.1
  52.1 0.3 convolution_subtract_fusion.2
  52.4 0.3 multiply_add_fusion
  52.7 0.3 fusion.62
  53.3 0.3 convolution_subtract_fusion
  53.5 0.3 convolution_add_fusion
  54.1 0.8 fusion.34
  55.2 24.8 %all_to_all.27 = f32[128,1,128]{2,1,0:T(1,128)S(1)} all-to-all(f32[128,1,128]{2,1,0:T(1,128)S(1)} %bitcast.52), channel_id=1, replica_groups=mesh['seq'=128,'ch'=4] {'seq'}, dimensions={0} | all-to-all | bytes 131072 | tf_op jit(solution)/shard_map/all_to_all | solution.py:97
  79.9 0.5 broadcast.67
  80.4 0.8 reduce.4
  81.3 7.8 %all_to_all.28 = f32[4,1,256]{2,1,0:T(1,128)S(1)} all-to-all(f32[4,1,256]{2,1,0:T(1,128)S(1)} %broadcast_in_dim.61), channel_id=1, replica_groups=mesh['seq'=128,'ch'=4] {'ch'}, dimensions={0} | all-to-all | bytes 8192 | tf_op jit(solution)/shard_map/all_to_all | solution.py:103
  89.2 0.6 multiply_multiply_fusion
  (30 shorter events, 2.0 us)
Async XLA Ops:
  0.0 28.3 %copy-start = (f32[7,64]{1,0:T(8,128)S(1)}, f32[7,64]{1,0:T(8,128)}, u32[]{:S(2)}) copy-start(f32[7,64]{1,0:T(8,128)} %param.8) | copy-start | bytes 5380
  0.0 0.8 copy-start.2
  0.0 0.9 copy-start.1
  1.9 42.1 %all-to-all-start = ((f32[128,1,256]{2,1,0:T(1,128)}), f32[128,1,256]{2,1,0:T(1,128)S(1)}, u32[]{:S(2)}, u32[]{:S(2)}) async-start(f32[128,1,256]{2,1,0:T(1,128)} %all_to_all.18), calls=%async_computation | async-start | bytes 262144 | tf_op jit(solution)/shard_map/all_to_all | solution.py:46
  27.0 0.7 copy-start.3
  44.0 5.1 %collective-permute-start.1 = (f32[64,256]{1,0:T(8,128)S(1)}, f32[64,256]{1,0:T(8,128)S(1)}, u32[]{:S(2)}, u32[]{:S(2)}) collective-permute-start(f32[64,256]{1,0:T(8,128)S(1)} %bitcast.54), channel_id=1, source_target_pairs={{0,4},{4,0},{8,12},{12,8},{16,20},{20,16},{24,28},{28,24},{32,36},... | collective-permute-start | bytes 196616 | tf_op jit(solution)/shard_map/ppermute | solution.py:50
  46.7 3.1 %collective-permute-start = (f32[64,256]{1,0:T(8,128)S(1)}, f32[64,256]{1,0:T(8,128)S(1)}, u32[]{:S(2)}, u32[]{:S(2)}) collective-permute-start(f32[64,256]{1,0:T(8,128)S(1)} %bitcast.55), channel_id=1, source_target_pairs={{0,4},{4,0},{8,12},{12,8},{16,20},{20,16},{24,28},{28,24},{32,36},... | collective-permute-start | bytes 196616 | tf_op jit(solution)/shard_map/ppermute | solution.py:49
